TPU v7x, 256 devices: a whole 4x4x8 slice. The times are simulated.
256 devices in a mesh: island: 4 (over x_lo, core), fsdp: 64 (over x_hi, z, y).
Axes of the slice: x: 4 (x_hi: 2, x_lo: 2; x = x_hi * 2 + x_lo), y: 4, z: 8, core: 2. Of those that a mesh axis runs over, the one named last changes fastest.
Arguments:
- acts: bfloat16 [65536, 8192], P(('island', 'fsdp')), may hold values from -24 to 24
- cotangent: bfloat16 [65536, 512], P(('island', 'fsdp')), may hold values from -6 to 6
- global_params: float32 [8192, 512], P('fsdp'), may hold values from -0.12 to 0.12
- momentum: float32 [8192, 512], P('fsdp'), may hold values from -0.18 to 0.18
- island_drift: float32 [4, 8192, 512], P('island', 'fsdp'), may hold values from -0.12 to 0.12
- moment1: float32 [4, 8192, 512], P('island', 'fsdp'), may hold values from -6 to 6
- moment2: float32 [4, 8192, 512], P('island', 'fsdp'), may hold values from 0.05 to 1
Outputs:
- keys: bfloat16 [65536, 512], P(('island', 'fsdp'))
- new_global: float32 [8192, 512], P('fsdp')
- new_momentum: float32 [8192, 512], P('fsdp')
- moment1_out: float32 [4, 8192, 512], P('island', 'fsdp')
- moment2_out: float32 [4, 8192, 512], P('island', 'fsdp')
All inputs are finite; a program needn't handle non-finite values.
Results may differ from a plain program's by a relative error of at most 0.0049.
Values may be sent and summed in bfloat16 or wider, within the bound.
No kernel may reach another device: no remote copies, remote signals or barrier semaphores. Data moves between devices by JAX's collectives and lax.ppermute only.
A program may use at most 128 MiB of HBM per device.

v0:
```python
import jax
import jax.numpy as jnp
from jax import lax
from jax.sharding import PartitionSpec as P

D = 8192


beta_one = 0.9
beta_two = 0.95
epsilon = 1e-08
inner_rate = 0.05
decay_rate = 0.1
outer_rate = 0.7
nesterov = 0.9


def per_device(acts, cotangent, global_params, momentum, island_drift, moment1, moment2):
    fsdp_count = lax.axis_size("fsdp")
    island_count = lax.axis_size("island")
    scale = (acts.shape[0] * fsdp_count) ** (-0.5)
    grad = lax.psum_scatter(
        lax.dot_general(
            acts, cotangent, (((0,), (0,)), ((), ())), preferred_element_type=jnp.float32
        ),
        "fsdp",
        scatter_dimension=0,
        tiled=True,
    )
    grad = grad * scale
    drift = island_drift[0]
    first = beta_one * moment1[0] + (1.0 - beta_one) * grad
    second = beta_two * moment2[0] + (1.0 - beta_two) * grad * grad
    step = first / (jnp.sqrt(second) + epsilon) + decay_rate * (global_params - drift)
    pseudo = drift + inner_rate * step
    mean = lax.psum(pseudo, "island") / island_count
    new_momentum = nesterov * momentum + mean
    new_global = global_params - outer_rate * (mean + nesterov * new_momentum)
    weights = new_global.astype(jnp.bfloat16)
    keys = jnp.dot(
        acts,
        lax.all_gather(weights, "fsdp", axis=0, tiled=True),
        preferred_element_type=jnp.float32,
    )
    keys = (keys * D ** (-0.5)).astype(jnp.bfloat16)
    return (keys, new_global, new_momentum, first[None], second[None])


def solution(mesh):
    return jax.shard_map(
        per_device,
        mesh=mesh,
        in_specs=(
            P(("island", "fsdp"), None),
            P(("island", "fsdp"), None),
            P("fsdp", None),
            P("fsdp", None),
            P("island", "fsdp", None),
            P("island", "fsdp", None),
            P("island", "fsdp", None),
        ),
        out_specs=(
            P(("island", "fsdp"), None),
            P("fsdp", None),
            P("fsdp", None),
            P("island", "fsdp", None),
            P("island", "fsdp", None),
        ),
        check_vma=False,
    )
```

profile of v0, /device:TPU:1, one launch (start us, length us, event | category | flops | bytes accessed | tf_op | source)
XLA Modules:
  0.0 630.2 jit_solution(935737495468121115)
XLA Ops:
  7.2 0.0 copy-start
  7.2 0.0 reduce-scatter.2.cloned.1.call-start
  7.2 0.9 copy-done
  8.1 10.3 %fusion.8 = f32[8192,512]{1,0:T(8,128)} fusion(bf16[256,8192]{1,0:T(8,128)(2,1)} %param.7, bf16[256,512]{1,0:T(8,128)(2,1)S(1)} %copy-done), kind=kOutput, calls=%fused_computation.15 | convolution fusion | flops 2147483648 | bytes 21233664 | tf_op jit(solution)/shard_map/dot_general | solution.py:23
  18.4 0.0 copy-start.1
  18.4 0.0 copy-start.3
  18.4 0.0 copy-start.2
  18.5 0.0 reduce-scatter.2.cloned.1.call-update
  18.5 0.0 all-reduce.2.cloned.1.call-start
  18.5 358.2 %reduce-scatter.2.cloned.1.call-done = f32[128,512]{1,0:T(8,128)} async-done(((f32[8192,512]{1,0:T(8,128)}), f32[128,512]{1,0:T(8,128)}) %reduce-scatter.2.cloned.1.call-update) | async-done | bytes 262160 | tf_op jit(solution)/shard_map/reduce_scatter | solution.py:22
  376.7 0.0 copy-done.1
  376.7 0.0 copy-done.3
  376.7 0.0 copy-done.4
  376.7 0.0 copy-done.5
  376.7 2.0 fusion.6
  378.7 0.0 all-reduce.2.cloned.1.call-update
  378.7 0.0 all-gather.2.cloned.1.call-start
  378.8 85.6 %all-reduce.2.cloned.1.call-done = f32[128,512]{1,0:T(8,128)} async-done(((f32[128,512]{1,0:T(8,128)}), f32[128,512]{1,0:T(8,128)}) %all-reduce.2.cloned.1.call-update) | async-done | bytes 262160 | tf_op jit(solution)/shard_map/psum | solution.py:36
  464.4 0.0 copy-done.2
  464.4 1.9 fusion.7
  466.3 0.0 all-gather.2.cloned.1.call-update
  466.3 149.6 %all-gather.2.cloned.1.call-done = bf16[8192,512]{1,0:T(8,128)(2,1)} async-done(((bf16[128,512]{1,0:T(8,128)(2,1)}), bf16[8192,512]{1,0:T(8,128)(2,1)}) %all-gather.2.cloned.1.call-update) | async-done | bytes 8388624 | tf_op jit(solution)/shard_map/all_gather | solution.py:42
  615.9 6.9 %fusion.1 = bf16[256,512]{0,1:T(8,128)(2,1)S(1)} fusion(bf16[8192,512]{1,0:T(8,128)(2,1)} %all-gather.2.cloned.1.call-done, bf16[256,8192]{1,0:T(8,128)(2,1)} %param.7), kind=kOutput, calls=%fused_computation.2 | convolution fusion | flops 2147745792 | bytes 12845056 | tf_op jit(solution)/shard_map/dot_general | solution.py:40
  622.8 0.8 copy.12
  (2 shorter events, 0.0 us)
Async XLA Ops:
  7.2 1.0 copy-start
  7.2 369.5 %reduce-scatter.2.cloned.1.call-start = ((), (), s32[]{:S(2)}) async-start(), calls=%async_computation.1 | async-start | bytes 17039360 | tf_op jit(solution)/shard_map/reduce_scatter | solution.py:22
  18.4 358.3 %copy-start.1 = (f32[128,512]{1,0:T(8,128)S(1)}, f32[128,512]{1,0:T(8,128)}, u32[]{:S(2)}) copy-start(f32[128,512]{1,0:T(8,128)} %param.9) | copy-start | bytes 786436
  18.4 358.3 %copy-start.3 = (f32[1,128,512]{2,1,0:T(8,128)S(1)}, f32[1,128,512]{2,1,0:T(8,128)}, u32[]{:S(2)}) copy-start(f32[1,128,512]{2,1,0:T(8,128)} %param.13) | copy-start | bytes 786436
  18.4 358.3 %copy-start.4 = (f32[1,128,512]{2,1,0:T(8,128)S(1)}, f32[1,128,512]{2,1,0:T(8,128)}, u32[]{:S(2)}) copy-start(f32[1,128,512]{2,1,0:T(8,128)} %param.12) | copy-start | bytes 786436
  18.4 358.3 %copy-start.5 = (f32[1,128,512]{2,1,0:T(8,128)S(1)}, f32[1,128,512]{2,1,0:T(8,128)}, u32[]{:S(2)}) copy-start(f32[1,128,512]{2,1,0:T(8,128)} %param.11) | copy-start | bytes 786436
  18.4 445.9 %copy-start.2 = (f32[128,512]{1,0:T(8,128)S(1)}, f32[128,512]{1,0:T(8,128)}, u32[]{:S(2)}) copy-start(f32[128,512]{1,0:T(8,128)} %param.10) | copy-start | bytes 786436
  18.5 445.9 %all-reduce.2.cloned.1.call-start = ((), (), s32[]{:S(2)}) async-start(), calls=%async_computation.2 | async-start | bytes 524288 | tf_op jit(solution)/shard_map/psum | solution.py:36
  378.7 237.1 %all-gather.2.cloned.1.call-start = ((), (), s32[]{:S(2)}) async-start(), calls=%async_computation.3 | async-start | bytes 8519680 | tf_op jit(solution)/shard_map/all_gather | solution.py:42
Sparse Core Ops, SparseCore 0:
  18.6 358.0 reduce-scatter.1
  379.9 84.4 all-reduce.1
  468.6 147.2 all-gather.1
where the time goes:
time: 633 us; the launch traced here: 630 us
  waiting for transfers between devices  593 us (94%)
  matrix products  17.2 us (3%)
  between operations  13.8 us (2%)
    reduce_scatter x1, waiting for transfers between devices, per_device(): lax.psum_scatter(lax.dot_general(acts, cotangent, (((0,), (0,)), ((), ())...  358 us
    all_gather x1, waiting for transfers between devices, per_device(): lax.all_gather(weights, 'fsdp', axis=0, tiled=True)  150 us
    psum x1, waiting for transfers between devices, per_device(): mean = lax.psum(pseudo, 'island') / island_count  85.6 us
  transfers between devices with their start and end apart: 3, of which 3 were waited for; matrix products, arithmetic and copies ran while one was open for 0% of the time, Pallas kernels for 0%

commit v1 on v0

v1 whole, which is shorter than its diff:
```python
import jax
import jax.numpy as jnp
from jax import lax
from jax.sharding import Mesh, PartitionSpec as P

D = 8192
FS = ("xh", "z", "y")


beta_one = 0.9
beta_two = 0.95
epsilon = 1e-08
inner_rate = 0.05
decay_rate = 0.1
outer_rate = 0.7
nesterov = 0.9


def per_device(acts, cotangent, global_params, momentum, island_drift, moment1, moment2):
    fsdp_count = lax.axis_size(FS)
    island_count = lax.axis_size("island")
    scale = (acts.shape[0] * fsdp_count) ** (-0.5)
    xh_n, z_n, y_n = (lax.axis_size(a) for a in ("xh", "z", "y"))
    tokens = acts.shape[0]
    acts_perm = (
        acts.reshape(tokens, xh_n, z_n, D // (xh_n * z_n))
        .transpose(0, 2, 1, 3)
        .reshape(tokens, D)
    )
    partial = lax.dot_general(
        acts_perm, cotangent, (((0,), (0,)), ((), ())), preferred_element_type=jnp.float32
    )
    grad = lax.psum_scatter(partial, "z", scatter_dimension=0, tiled=True)
    grad = lax.psum_scatter(grad, "xh", scatter_dimension=0, tiled=True)
    grad = lax.psum_scatter(grad, "y", scatter_dimension=0, tiled=True)
    grad = grad * scale
    drift = island_drift[0]
    first = beta_one * moment1[0] + (1.0 - beta_one) * grad
    second = beta_two * moment2[0] + (1.0 - beta_two) * grad * grad
    step = first / (jnp.sqrt(second) + epsilon) + decay_rate * (global_params - drift)
    pseudo = drift + inner_rate * step
    pair_core = [(i, i ^ 1) for i in range(island_count)]
    pair_chip = [(i, i ^ 2) for i in range(island_count)]
    summed = pseudo + lax.ppermute(pseudo, "island", pair_core)
    summed = summed + lax.ppermute(summed, "island", pair_chip)
    mean = summed / island_count
    new_momentum = nesterov * momentum + mean
    new_global = global_params - outer_rate * (mean + nesterov * new_momentum)
    weights = new_global.astype(jnp.bfloat16)
    core = lax.axis_index("island") % 2
    half = weights.shape[1] // 2
    own = lax.dynamic_slice_in_dim(weights, core * half, half, axis=1)
    own_full = lax.all_gather(own, FS, axis=0, tiled=True)
    other_full = lax.ppermute(own_full, "island", pair_core)
    keys_own = jnp.dot(acts, own_full, preferred_element_type=jnp.float32)
    keys_other = jnp.dot(acts, other_full, preferred_element_type=jnp.float32)
    keys_own = (keys_own * D ** (-0.5)).astype(jnp.bfloat16)
    keys_other = (keys_other * D ** (-0.5)).astype(jnp.bfloat16)
    is_first = core == 0
    keys = jnp.concatenate(
        [jnp.where(is_first, keys_own, keys_other), jnp.where(is_first, keys_other, keys_own)],
        axis=1,
    )
    return (keys, new_global, new_momentum, first[None], second[None])


def solution(mesh):
    fsdp_n = mesh.shape["fsdp"]
    mesh = Mesh(mesh.devices.reshape(mesh.shape["island"], 2, 8, fsdp_n // 16), ("island",) + FS)
    return jax.shard_map(
        per_device,
        mesh=mesh,
        in_specs=(
            P(("island", *FS), None),
            P(("island", *FS), None),
            P(FS, None),
            P(FS, None),
            P("island", FS, None),
            P("island", FS, None),
            P("island", FS, None),
        ),
        out_specs=(
            P(("island", *FS), None),
            P(FS, None),
            P(FS, None),
            P("island", FS, None),
            P("island", FS, None),
        ),
        check_vma=False,
    )
```

time: 633 us -> 432 us (0.68)
  waiting for transfers between devices: 593 us -> 383 us
  local copies, waits for them, and re-layouts: 1.77 us -> 10.4 us
  starting transfers between devices: 0.12 us -> 7.87 us
    reduce_scatter x1 -> x3, waiting for transfers between devices: 358 us -> 244 us  [the longest x1 177 us: per_device(): grad = lax.psum_scatter(partial, 'z', scatter_dimension=0, tiled=True)]
    psum x1 -> x0, waiting for transfers between devices: 85.6 us -> none  [per_device(): mean = lax.psum(pseudo, 'island') / island_count]
    all_gather x1, waiting for transfers between devices: 150 us -> 124 us  [per_device(): own_full = lax.all_gather(own, FS, axis=0, tiled=True)]
    ppermute x0 -> x3, waiting for transfers between devices: none -> 14.6 us  [the longest x1 7.12 us: per_device(): other_full = lax.ppermute(own_full, 'island', pair_core)]
    ppermute x0 -> x3, starting transfers between devices: none -> 7.72 us  [the longest x1 4.24 us: per_device(): other_full = lax.ppermute(own_full, 'island', pair_core)]
    dot_general x2 -> x3, matrix products: 17.2 us -> 14.2 us  [the longest x1 8.1 us: per_device(): lax.dot_general(acts_perm, cotangent, (((0,), (0,)), ((), ())), preferred...]
  transfers between devices with their start and end apart: 3 -> 7, of which waited for: 3 -> 7; matrix products, arithmetic and copies ran while one was open for 0% -> 0% of each run, Pallas kernels for 0% -> 0%
where the time goes in v1:
time: 432 us
  waiting for transfers between devices  383 us (89%)
  matrix products  14.2 us (3%)
  between operations  13.9 us (3%)
  local copies, waits for them, and re-layouts  10.4 us (2%)
  starting transfers between devices  7.87 us (2%)
    reduce_scatter x1, waiting for transfers between devices, per_device(): grad = lax.psum_scatter(partial, 'z', scatter_dimension=0, tiled=True)  177 us
    all_gather x1, waiting for transfers between devices, per_device(): own_full = lax.all_gather(own, FS, axis=0, tiled=True)  124 us
    reduce_scatter x1, waiting for transfers between devices, per_device(): grad = lax.psum_scatter(grad, 'xh', scatter_dimension=0, tiled=True)  39.5 us
    reduce_scatter x1, waiting for transfers between devices, per_device(): grad = lax.psum_scatter(grad, 'y', scatter_dimension=0, tiled=True)  27 us
  transfers between devices with their start and end apart: 7, of which 7 were waited for; matrix products, arithmetic and copies ran while one was open for 0% of the time, Pallas kernels for 0%

profile of v1, /device:TPU:1, one launch (start us, length us, event | category | flops | bytes accessed | tf_op | source)
XLA Modules:
  0.0 432.0 jit_solution(1409496534043252752)
XLA Ops:
  7.2 0.0 reduce-scatter.4.cloned.1.call-start
  7.2 6.4 %copy.14 = bf16[256,8192]{0,1:T(8,128)(2,1)} copy(bf16[256,8192]{1,0:T(8,128)(2,1)} %param.7) | data formatting | bytes 8388608 | tf_op args[0]
  13.6 2.5 copy.15
  16.1 8.1 %fusion.7 = f32[8192,512]{1,0:T(8,128)} fusion(bf16[256,8192]{0,1:T(8,128)(2,1)S(1)} %bitcast.42, bf16[256,512]{1,0:T(8,128)(2,1)S(1)} %copy-done), kind=kOutput, calls=%fused_computation.20 | convolution fusion | flops 2147483648 | bytes 21233664 | tf_op jit(solution)/shard_map/dot_general | solution.py:30
  24.2 0.0 reduce-scatter.4.cloned.1.call-update
  24.3 0.0 reduce-scatter.6.cloned.1.call-start
  24.3 177.4 %reduce-scatter.4.cloned.1.call-done = f32[1024,512]{1,0:T(8,128)} async-done(((f32[8192,512]{1,0:T(8,128)}), f32[1024,512]{1,0:T(8,128)}) %reduce-scatter.4.cloned.1.call-update) | async-done | bytes 2097168 | tf_op jit(solution)/shard_map/reduce_scatter | solution.py:33
  201.7 0.0 reduce-scatter.8.cloned.1.call-start
  201.8 39.5 %reduce-scatter.6.cloned.1.call-done = f32[512,512]{1,0:T(8,128)} async-done(((f32[1024,512]{1,0:T(8,128)}), f32[512,512]{1,0:T(8,128)}) %reduce-scatter.6.cloned.1.call-update) | async-done | bytes 1048592 | tf_op jit(solution)/shard_map/reduce_scatter | solution.py:34
  241.2 0.0 all-gather.2.cloned.1.call-start
  241.3 27.0 %reduce-scatter.8.cloned.1.call-done = f32[128,512]{1,0:T(8,128)} async-done(((f32[512,512]{1,0:T(8,128)}), f32[128,512]{1,0:T(8,128)}) %reduce-scatter.8.cloned.1.call-update) | async-done | bytes 262160 | tf_op jit(solution)/shard_map/reduce_scatter | solution.py:35
  268.3 1.9 fusion.6
  270.2 2.2 collective-permute-start
  272.4 1.2 collective-permute-done
  273.6 1.3 collective-permute-start.1
  274.9 6.3 %collective-permute-done.1 = f32[128,512]{1,0:T(8,128)S(1)} collective-permute-done((f32[128,512]{1,0:T(8,128)S(1)}, f32[128,512]{1,0:T(8,128)S(1)}, u32[]{:S(2)}, u32[]{:S(2)}) %collective-permute-start.1) | collective-permute-done | bytes 262176 | tf_op jit(solution)/shard_map/ppermute | solution.py:45
  281.2 0.8 multiply_subtract_fusion
  282.0 0.7 dynamic-slice_convert_fusion
  282.8 124.4 %all-gather.2.cloned.1.call-done = bf16[8192,256]{1,0:T(8,128)(2,1)} async-done(((bf16[128,256]{1,0:T(8,128)(2,1)}), bf16[8192,256]{1,0:T(8,128)(2,1)}) %all-gather.2.cloned.1.call-update) | async-done | bytes 4194320 | tf_op jit(solution)/shard_map/all_gather | solution.py:53
  407.1 4.2 collective-permute-start.2
  411.4 7.1 %collective-permute-done.2 = bf16[8192,256]{1,0:T(8,128)(2,1)} collective-permute-done((bf16[8192,256]{1,0:T(8,128)(2,1)}, bf16[8192,256]{1,0:T(8,128)(2,1)}, u32[]{:S(2)}, u32[]{:S(2)}) %collective-permute-start.2) | collective-permute-done | bytes 4194336 | tf_op jit(solution)/shard_map/ppermute | solution.py:54
  418.5 4.8 %fusion.1 = bf16[256,256]{1,0:T(8,128)(2,1)S(1)} fusion(bf16[8192,256]{1,0:T(8,128)(2,1)} %collective-permute-done.2, bf16[256,8192]{1,0:T(8,128)(2,1)} %param.7), kind=kOutput, calls=%fused_computation.3 | convolution fusion | flops 1073872896 | bytes 8519680 | tf_op jit(solution)/shard_map/dot_general | solution.py:56
  423.3 1.3 select_bitcast_fusion.1
  424.6 0.8 copy.16
  (23 shorter events, 0.2 us)
Async XLA Ops:
  7.2 8.9 %copy-start = (bf16[256,512]{1,0:T(8,128)(2,1)S(1)}, bf16[256,512]{1,0:T(8,128)(2,1)}, u32[]{:S(2)}) copy-start(bf16[256,512]{1,0:T(8,128)(2,1)} %param.8) | copy-start | bytes 786436
  7.2 194.5 %reduce-scatter.4.cloned.1.call-start = ((), (), s32[]{:S(2)}) async-start(), calls=%async_computation.3 | async-start | bytes 18874368 | tf_op jit(solution)/shard_map/reduce_scatter | solution.py:33
  24.2 244.1 %copy-start.2 = (f32[128,512]{1,0:T(8,128)S(1)}, f32[128,512]{1,0:T(8,128)}, u32[]{:S(2)}) copy-start(f32[128,512]{1,0:T(8,128)} %param.9) | copy-start | bytes 786436
  24.2 244.1 %copy-start.5 = (f32[1,128,512]{2,1,0:T(8,128)S(1)}, f32[1,128,512]{2,1,0:T(8,128)}, u32[]{:S(2)}) copy-start(f32[1,128,512]{2,1,0:T(8,128)} %param.13) | copy-start | bytes 786436
  24.2 244.1 %copy-start.6 = (f32[1,128,512]{2,1,0:T(8,128)S(1)}, f32[1,128,512]{2,1,0:T(8,128)}, u32[]{:S(2)}) copy-start(f32[1,128,512]{2,1,0:T(8,128)} %param.12) | copy-start | bytes 786436
  24.2 244.1 %copy-start.7 = (f32[1,128,512]{2,1,0:T(8,128)S(1)}, f32[1,128,512]{2,1,0:T(8,128)}, u32[]{:S(2)}) copy-start(f32[1,128,512]{2,1,0:T(8,128)} %param.11) | copy-start | bytes 786436
  24.2 257.0 %copy-start.4 = (f32[128,512]{1,0:T(8,128)S(1)}, f32[128,512]{1,0:T(8,128)}, u32[]{:S(2)}) copy-start(f32[128,512]{1,0:T(8,128)} %param.10) | copy-start | bytes 786436
  24.3 217.0 %reduce-scatter.6.cloned.1.call-start = ((), (), s32[]{:S(2)}) async-start(), calls=%async_computation.4 | async-start | bytes 3145728 | tf_op jit(solution)/shard_map/reduce_scatter | solution.py:34
  201.7 66.6 %reduce-scatter.8.cloned.1.call-start = ((), (), s32[]{:S(2)}) async-start(), calls=%async_computation.5 | async-start | bytes 1310720 | tf_op jit(solution)/shard_map/reduce_scatter | solution.py:35
  241.2 165.9 %all-gather.2.cloned.1.call-start = ((), (), s32[]{:S(2)}) async-start(), calls=%async_computation.6 | async-start | bytes 4259840 | tf_op jit(solution)/shard_map/all_gather | solution.py:53
  270.2 3.4 collective-permute-start
  273.6 7.6 %collective-permute-start.1 = (f32[128,512]{1,0:T(8,128)S(1)}, f32[128,512]{1,0:T(8,128)S(1)}, u32[]{:S(2)}, u32[]{:S(2)}) collective-permute-start(f32[128,512]{1,0:T(8,128)S(1)} %add.50), channel_id=1, source_target_pairs={{0,128},{64,192},{128,0},{192,64},{1,129},{65,193},{129,1},{193,65... | collective-permute-start | bytes 786440 | tf_op jit(solution)/shard_map/ppermute | solution.py:45
  282.0 141.2 %copy-start.3 = (f32[128,512]{1,0:T(8,128)}, f32[128,512]{1,0:T(8,128)S(1)}, u32[]{:S(2)}) copy-start(f32[128,512]{1,0:T(8,128)S(1)} %get-tuple-element.20) | copy-start | bytes 786436
  407.1 11.4 %collective-permute-start.2 = (bf16[8192,256]{1,0:T(8,128)(2,1)}, bf16[8192,256]{1,0:T(8,128)(2,1)}, u32[]{:S(2)}, u32[]{:S(2)}) collective-permute-start(bf16[8192,256]{1,0:T(8,128)(2,1)} %all-gather.2.cloned.1.call-done), channel_id=1, source_target_pairs={{0,64},{64,0},{128,192},{192,128},{1,65},{65,1},{129,193},{193,129... | collective-permute-start | bytes 12582920 | tf_op jit(solution)/shard_map/ppermute | solution.py:54
  411.3 11.9 %copy-start.1 = (bf16[256,8192]{1,0:T(8,128)(2,1)S(1)}, bf16[256,8192]{1,0:T(8,128)(2,1)}, u32[]{:S(2)}) copy-start(bf16[256,8192]{1,0:T(8,128)(2,1)} %param.7) | copy-start | bytes 12582916
  411.3 11.9 %copy-start.8 = (bf16[8192,256]{1,0:T(8,128)(2,1)S(1)}, bf16[8192,256]{1,0:T(8,128)(2,1)}, u32[]{:S(2)}) copy-start(bf16[8192,256]{1,0:T(8,128)(2,1)} %all-gather.2.cloned.1.call-done) | copy-start | bytes 12582916
Sparse Core Ops, SparseCore 0:
  24.4 177.2 reduce-scatter.3
  204.2 36.9 reduce-scatter.5
  243.8 24.4 reduce-scatter.7
  282.9 124.1 all-gather.1

commit v2 on v1

--- a/solution.py
+++ b/solution.py
@@ -50,10 +50,12 @@
     core = lax.axis_index("island") % 2
     half = weights.shape[1] // 2
     own = lax.dynamic_slice_in_dim(weights, core * half, half, axis=1)
-    own_full = lax.all_gather(own, FS, axis=0, tiled=True)
+    own_full = lax.all_gather(own, "y", axis=0, tiled=True)
+    own_full = lax.all_gather(own_full, "xh", axis=0, tiled=True)
+    own_full = lax.all_gather(own_full, "z", axis=0, tiled=True)
     other_full = lax.ppermute(own_full, "island", pair_core)
-    keys_own = jnp.dot(acts, own_full, preferred_element_type=jnp.float32)
-    keys_other = jnp.dot(acts, other_full, preferred_element_type=jnp.float32)
+    keys_own = jnp.dot(acts_perm, own_full, preferred_element_type=jnp.float32)
+    keys_other = jnp.dot(acts_perm, other_full, preferred_element_type=jnp.float32)
     keys_own = (keys_own * D ** (-0.5)).astype(jnp.bfloat16)
     keys_other = (keys_other * D ** (-0.5)).astype(jnp.bfloat16)
     is_first = core == 0

time: 432 us -> 379 us (0.88)
  waiting for transfers between devices: 383 us -> 313 us
  blocking collectives: 0 us -> 16.9 us
    all_gather x1, waiting for transfers between devices: 124 us -> 59 us  [per_device(): own_full = lax.all_gather(own_full, 'z', axis=0, tiled=True)]
    all_gather x0 -> x2, blocking collectives: none -> 16.9 us  [the longest x1 9.37 us: per_device(): own_full = lax.all_gather(own, 'y', axis=0, tiled=True)]
    ppermute x1, waiting for transfers between devices: 7.12 us -> 2.21 us  [per_device(): other_full = lax.ppermute(own_full, 'island', pair_core)]
  transfers between devices with their start and end apart: 7 -> 7, of which waited for: 7 -> 7; matrix products, arithmetic and copies ran while one was open for 0% -> 1% of each run, Pallas kernels for 0% -> 0%
where the time goes in v2:
time: 379 us
  waiting for transfers between devices  313 us (83%)
  blocking collectives  16.9 us (4%)
  matrix products  16.5 us (4%)
  between operations  13.8 us (4%)
  local copies, waits for them, and re-layouts  11.7 us (3%)
  starting transfers between devices  4.4 us (1%)
    reduce_scatter x1, waiting for transfers between devices, per_device(): grad = lax.psum_scatter(partial, 'z', scatter_dimension=0, tiled=True)  177 us
    all_gather x1, waiting for transfers between devices, per_device(): own_full = lax.all_gather(own_full, 'z', axis=0, tiled=True)  59 us
    reduce_scatter x1, waiting for transfers between devices, per_device(): grad = lax.psum_scatter(grad, 'xh', scatter_dimension=0, tiled=True)  39.5 us
    reduce_scatter x1, waiting for transfers between devices, per_device(): grad = lax.psum_scatter(grad, 'y', scatter_dimension=0, tiled=True)  27 us
    all_gather x1, blocking collectives, per_device(): own_full = lax.all_gather(own, 'y', axis=0, tiled=True)  9.37 us
    unnamed x20, local copies, waits for them, and re-layouts  9.24 us
    dot_general x1, matrix products, per_device(): lax.dot_general(acts_perm, cotangent, (((0,), (0,)), ((), ())), preferred...  8.09 us
  transfers between devices with their start and end apart: 7, of which 7 were waited for; matrix products, arithmetic and copies ran while one was open for 1% of the time, Pallas kernels for 0%

profile of v2, /device:TPU:1, one launch (start us, length us, event | category | flops | bytes accessed | tf_op | source)
XLA Modules:
  0.0 378.8 jit_solution(14514594827470282535)
XLA Ops:
  7.2 6.4 %copy.14 = bf16[256,8192]{0,1:T(8,128)(2,1)} copy(bf16[256,8192]{1,0:T(8,128)(2,1)} %param.7) | data formatting | bytes 8388608 | tf_op args[0]
  13.6 2.5 copy.15
  16.1 1.9 copy-done.1
  18.1 8.1 %fusion.7 = f32[8192,512]{1,0:T(8,128)} fusion(bf16[256,8192]{0,1:T(8,128)(2,1)S(1)} %bitcast.41, bf16[256,512]{1,0:T(8,128)(2,1)S(1)} %copy-done), kind=kOutput, calls=%fused_computation.20 | convolution fusion | flops 2147483648 | bytes 21233664 | tf_op jit(solution)/shard_map/dot_general | solution.py:30
  26.2 0.0 reduce-scatter.6.cloned.1.call-start
  26.2 177.4 %reduce-scatter.4.cloned.1.call-done = f32[1024,512]{1,0:T(8,128)} async-done(((f32[8192,512]{1,0:T(8,128)}), f32[1024,512]{1,0:T(8,128)}) %reduce-scatter.4.cloned.1.call-update) | async-done | bytes 2097168 | tf_op jit(solution)/shard_map/reduce_scatter | solution.py:33
  203.7 0.0 reduce-scatter.8.cloned.1.call-start
  203.7 39.5 %reduce-scatter.6.cloned.1.call-done = f32[512,512]{1,0:T(8,128)} async-done(((f32[1024,512]{1,0:T(8,128)}), f32[512,512]{1,0:T(8,128)}) %reduce-scatter.6.cloned.1.call-update) | async-done | bytes 1048592 | tf_op jit(solution)/shard_map/reduce_scatter | solution.py:34
  243.2 0.0 all-gather.2.cloned.1.call-start
  243.2 27.0 %reduce-scatter.8.cloned.1.call-done = f32[128,512]{1,0:T(8,128)} async-done(((f32[512,512]{1,0:T(8,128)}), f32[128,512]{1,0:T(8,128)}) %reduce-scatter.8.cloned.1.call-update) | async-done | bytes 262160 | tf_op jit(solution)/shard_map/reduce_scatter | solution.py:35
  270.2 1.9 fusion.6
  272.2 2.2 collective-permute-start
  274.4 1.2 collective-permute-done
  275.6 1.2 collective-permute-start.1
  276.8 6.4 %collective-permute-done.1 = f32[128,512]{1,0:T(8,128)S(1)} collective-permute-done((f32[128,512]{1,0:T(8,128)S(1)}, f32[128,512]{1,0:T(8,128)S(1)}, u32[]{:S(2)}, u32[]{:S(2)}) %collective-permute-start.1) | collective-permute-done | bytes 262176 | tf_op jit(solution)/shard_map/ppermute | solution.py:45
  283.1 0.8 multiply_subtract_fusion
  284.0 9.4 %all_gather.9 = bf16[512,256]{1,0:T(8,128)(2,1)S(1)} all-gather(bf16[128,256]{1,0:T(8,128)(2,1)S(1)} %dynamic-slice_convert_fusion), channel_id=1, replica_groups=mesh['island'=4,'xh'=2,'z'=8,'y'=4] {'y'}, dimensions={0}, use_global_device_ids=true | all-gather | bytes 327680 | tf_op jit(solution)/shard_map/all_gather | solution.py:53
  293.3 7.5 %all_gather.10 = bf16[1024,256]{1,0:T(8,128)(2,1)} all-gather(bf16[512,256]{1,0:T(8,128)(2,1)S(1)} %all_gather.9), channel_id=1, replica_groups=mesh['island'=4,'xh'=2,'z'=8,'y'=4] {'xh'}, dimensions={0}, use_global_device_ids=true | all-gather | bytes 786432 | tf_op jit(solution)/shard_map/all_gather | solution.py:54
  300.8 59.0 %all-gather.2.cloned.1.call-done = bf16[8192,256]{1,0:T(8,128)(2,1)} async-done(((bf16[1024,256]{1,0:T(8,128)(2,1)}), bf16[8192,256]{1,0:T(8,128)(2,1)}) %all-gather.2.cloned.1.call-update) | async-done | bytes 4194320 | tf_op jit(solution)/shard_map/all_gather | solution.py:55
  359.9 0.8 collective-permute-start.2
  360.7 4.9 %fusion = bf16[256,256]{1,0:T(8,128)(2,1)S(1)} fusion(bf16[8192,256]{1,0:T(8,128)(2,1)} %all-gather.2.cloned.1.call-done, bf16[256,8192]{0,1:T(8,128)(2,1)} %bitcast.42), kind=kOutput, calls=%fused_computation.2 | convolution fusion | flops 1073872896 | bytes 8519680 | tf_op jit(solution)/shard_map/dot_general | solution.py:57
  365.6 2.2 collective-permute-done.2
  367.8 3.5 select_bitcast_fusion.1
  371.4 0.8 copy.16
  (25 shorter events, 0.2 us)
Async XLA Ops:
  7.2 10.9 %copy-start = (bf16[256,512]{1,0:T(8,128)(2,1)S(1)}, bf16[256,512]{1,0:T(8,128)(2,1)}, u32[]{:S(2)}) copy-start(bf16[256,512]{1,0:T(8,128)(2,1)} %param.8) | copy-start | bytes 786436
  7.2 196.4 %reduce-scatter.4.cloned.1.call-start = ((), (), s32[]{:S(2)}) async-start(), calls=%async_computation.3 | async-start | bytes 18874368 | tf_op jit(solution)/shard_map/reduce_scatter | solution.py:33
  16.1 2.0 copy-start.1
  26.1 244.1 %copy-start.3 = (f32[128,512]{1,0:T(8,128)S(1)}, f32[128,512]{1,0:T(8,128)}, u32[]{:S(2)}) copy-start(f32[128,512]{1,0:T(8,128)} %param.9) | copy-start | bytes 786436
  26.2 244.1 %copy-start.6 = (f32[1,128,512]{2,1,0:T(8,128)S(1)}, f32[1,128,512]{2,1,0:T(8,128)}, u32[]{:S(2)}) copy-start(f32[1,128,512]{2,1,0:T(8,128)} %param.13) | copy-start | bytes 786436
  26.2 244.1 %copy-start.7 = (f32[1,128,512]{2,1,0:T(8,128)S(1)}, f32[1,128,512]{2,1,0:T(8,128)}, u32[]{:S(2)}) copy-start(f32[1,128,512]{2,1,0:T(8,128)} %param.12) | copy-start | bytes 786436
  26.2 244.1 %copy-start.8 = (f32[1,128,512]{2,1,0:T(8,128)S(1)}, f32[1,128,512]{2,1,0:T(8,128)}, u32[]{:S(2)}) copy-start(f32[1,128,512]{2,1,0:T(8,128)} %param.11) | copy-start | bytes 786436
  26.2 257.0 %copy-start.5 = (f32[128,512]{1,0:T(8,128)S(1)}, f32[128,512]{1,0:T(8,128)}, u32[]{:S(2)}) copy-start(f32[128,512]{1,0:T(8,128)} %param.10) | copy-start | bytes 786436
  26.2 217.0 %reduce-scatter.6.cloned.1.call-start = ((), (), s32[]{:S(2)}) async-start(), calls=%async_computation.4 | async-start | bytes 3145728 | tf_op jit(solution)/shard_map/reduce_scatter | solution.py:34
  203.7 66.6 %reduce-scatter.8.cloned.1.call-start = ((), (), s32[]{:S(2)}) async-start(), calls=%async_computation.5 | async-start | bytes 1310720 | tf_op jit(solution)/shard_map/reduce_scatter | solution.py:35
  243.2 116.7 %all-gather.2.cloned.1.call-start = ((), (), s32[]{:S(2)}) async-start(), calls=%async_computation.6 | async-start | bytes 4718592 | tf_op jit(solution)/shard_map/all_gather | solution.py:55
  272.2 3.4 collective-permute-start
  275.6 7.6 %collective-permute-start.1 = (f32[128,512]{1,0:T(8,128)S(1)}, f32[128,512]{1,0:T(8,128)S(1)}, u32[]{:S(2)}, u32[]{:S(2)}) collective-permute-start(f32[128,512]{1,0:T(8,128)S(1)} %add.50), channel_id=1, source_target_pairs={{0,128},{64,192},{128,0},{192,64},{1,129},{65,193},{129,1},{193,65... | collective-permute-start | bytes 786440 | tf_op jit(solution)/shard_map/ppermute | solution.py:45
  283.9 81.7 %copy-start.4 = (f32[128,512]{1,0:T(8,128)}, f32[128,512]{1,0:T(8,128)S(1)}, u32[]{:S(2)}) copy-start(f32[128,512]{1,0:T(8,128)S(1)} %get-tuple-element.20) | copy-start | bytes 786436
  359.9 8.0 %collective-permute-start.2 = (bf16[8192,256]{1,0:T(8,128)(2,1)}, bf16[8192,256]{1,0:T(8,128)(2,1)}, u32[]{:S(2)}, u32[]{:S(2)}) collective-permute-start(bf16[8192,256]{1,0:T(8,128)(2,1)} %all-gather.2.cloned.1.call-done), channel_id=1, source_target_pairs={{0,64},{64,0},{128,192},{192,128},{1,65},{65,1},{129,193},{193,129... | collective-permute-start | bytes 12582920 | tf_op jit(solution)/shard_map/ppermute | solution.py:56
  360.7 7.1 %copy-start.2 = (bf16[256,8,2,512]{0,3,2,1:T(8,128)(2,1)S(1)}, bf16[256,8,2,512]{0,3,2,1:T(8,128)(2,1)}, u32[]{:S(2)}) copy-start(bf16[256,8,2,512]{0,3,2,1:T(8,128)(2,1)} %copy-done.1) | copy-start | bytes 12582916
Sparse Core Ops, SparseCore 0:
  26.3 177.2 reduce-scatter.3
  206.1 36.9 reduce-scatter.5
  245.7 24.4 reduce-scatter.7
  301.0 58.8 all-gather.1

commit v3 on v2

--- a/solution.py
+++ b/solution.py
@@ -16,6 +16,33 @@
 nesterov = 0.9
 
 
+def halving_scatter(x, axis):
+    n = lax.axis_size(axis)
+    me = lax.axis_index(axis)
+    bit = n // 2
+    while bit >= 1:
+        half = x.shape[0] // 2
+        mine = (me // bit) % 2
+        keep = lax.dynamic_slice_in_dim(x, mine * half, half, axis=0)
+        send = lax.dynamic_slice_in_dim(x, (1 - mine) * half, half, axis=0)
+        recv = lax.ppermute(send, axis, [(i, i ^ bit) for i in range(n)])
+        x = keep + recv
+        bit //= 2
+    return x
+
+
+def doubling_gather(x, axis):
+    n = lax.axis_size(axis)
+    me = lax.axis_index(axis)
+    bit = 1
+    while bit < n:
+        recv = lax.ppermute(x, axis, [(i, i ^ bit) for i in range(n)])
+        low = (me // bit) % 2 == 0
+        x = jnp.where(low, jnp.concatenate([x, recv], 0), jnp.concatenate([recv, x], 0))
+        bit *= 2
+    return x
+
+
 def per_device(acts, cotangent, global_params, momentum, island_drift, moment1, moment2):
     fsdp_count = lax.axis_size(FS)
     island_count = lax.axis_size("island")
@@ -31,8 +58,8 @@
         acts_perm, cotangent, (((0,), (0,)), ((), ())), preferred_element_type=jnp.float32
     )
     grad = lax.psum_scatter(partial, "z", scatter_dimension=0, tiled=True)
-    grad = lax.psum_scatter(grad, "xh", scatter_dimension=0, tiled=True)
-    grad = lax.psum_scatter(grad, "y", scatter_dimension=0, tiled=True)
+    grad = halving_scatter(grad, "xh")
+    grad = halving_scatter(grad, "y")
     grad = grad * scale
     drift = island_drift[0]
     first = beta_one * moment1[0] + (1.0 - beta_one) * grad
@@ -50,8 +77,8 @@
     core = lax.axis_index("island") % 2
     half = weights.shape[1] // 2
     own = lax.dynamic_slice_in_dim(weights, core * half, half, axis=1)
-    own_full = lax.all_gather(own, "y", axis=0, tiled=True)
-    own_full = lax.all_gather(own_full, "xh", axis=0, tiled=True)
+    own_full = doubling_gather(own, "y")
+    own_full = doubling_gather(own_full, "xh")
     own_full = lax.all_gather(own_full, "z", axis=0, tiled=True)
     other_full = lax.ppermute(own_full, "island", pair_core)
     keys_own = jnp.dot(acts_perm, own_full, preferred_element_type=jnp.float32)

time: 379 us -> 362 us (0.955)
  waiting for transfers between devices: 313 us -> 295 us
  blocking collectives: 16.9 us -> 0 us
  starting transfers between devices: 4.4 us -> 19.6 us
    reduce_scatter x2 -> x0, waiting for transfers between devices: 66.4 us -> none  [the longest x1 39.5 us: per_device(): grad = lax.psum_scatter(grad, 'xh', scatter_dimension=0, tiled=True)]
    ppermute x0 -> x6, waiting for transfers between devices: none -> 46 us  [the longest x3 37.5 us: halving_scatter(): recv = lax.ppermute(send, axis, [(i, i ^ bit) for i in range(n)])]
    all_gather x2 -> x0, blocking collectives: 16.9 us -> none  [the longest x1 9.37 us: per_device(): own_full = lax.all_gather(own, 'y', axis=0, tiled=True)]
    ppermute x0 -> x6, starting transfers between devices: none -> 13.8 us  [the longest x3 6.89 us: doubling_gather(): recv = lax.ppermute(x, axis, [(i, i ^ bit) for i in range(n)])]
    ppermute x1, waiting for transfers between devices: 2.21 us -> 7.12 us  [per_device(): other_full = lax.ppermute(own_full, 'island', pair_core)]
  transfers between devices with their start and end apart: 7 -> 11, of which waited for: 7 -> 11; matrix products, arithmetic and copies ran while one was open for 1% -> 0% of each run, Pallas kernels for 0% -> 0%
where the time goes in v3:
time: 362 us
  waiting for transfers between devices  295 us (81%)
  starting transfers between devices  19.6 us (5%)
  between operations  14.2 us (4%)
  matrix products  14.1 us (4%)
  local copies, waits for them, and re-layouts  13.1 us (4%)
  other arithmetic  5.48 us (2%)
    reduce_scatter x1, waiting for transfers between devices, per_device(): grad = lax.psum_scatter(partial, 'z', scatter_dimension=0, tiled=True)  177 us
    all_gather x1, waiting for transfers between devices, per_device(): own_full = lax.all_gather(own_full, 'z', axis=0, tiled=True)  57.4 us
    ppermute x3, waiting for transfers between devices, halving_scatter(): recv = lax.ppermute(send, axis, [(i, i ^ bit) for i in range(n)])  37.5 us
    unnamed x20, local copies, waits for them, and re-layouts  9.23 us
    ppermute x3, waiting for transfers between devices, doubling_gather(): recv = lax.ppermute(x, axis, [(i, i ^ bit) for i in range(n)])  8.53 us
    dot_general x1, matrix products, per_device(): lax.dot_general(acts_perm, cotangent, (((0,), (0,)), ((), ())), preferred...  8.07 us
  transfers between devices with their start and end apart: 11, of which 11 were waited for; matrix products, arithmetic and copies ran while one was open for 0% of the time, Pallas kernels for 0%

profile of v3, /device:TPU:1, one launch (start us, length us, event | category | flops | bytes accessed | tf_op | source)
XLA Modules:
  0.0 361.8 jit_solution(179591686970727868)
XLA Ops:
  7.2 6.4 %copy.14 = bf16[256,8192]{0,1:T(8,128)(2,1)} copy(bf16[256,8192]{1,0:T(8,128)(2,1)} %param.7) | data formatting | bytes 8388608 | tf_op args[0]
  13.6 2.5 copy.15
  16.1 1.9 copy-done.1
  18.0 8.1 %fusion.5 = f32[8192,512]{1,0:T(8,128)} fusion(bf16[256,8192]{0,1:T(8,128)(2,1)S(1)} %bitcast.33, bf16[256,512]{1,0:T(8,128)(2,1)S(1)} %copy-done), kind=kOutput, calls=%fused_computation.27 | convolution fusion | flops 2147483648 | bytes 21233664 | tf_op jit(solution)/shard_map/dot_general | solution.py:57
  26.2 177.3 %reduce-scatter.2.cloned.1.call-done = f32[1024,512]{1,0:T(8,128)} async-done(((f32[8192,512]{1,0:T(8,128)}), f32[1024,512]{1,0:T(8,128)}) %reduce-scatter.2.cloned.1.call-update) | async-done | bytes 2097168 | tf_op jit(solution)/shard_map/reduce_scatter | solution.py:60
  204.9 2.8 collective-permute-start
  207.6 22.8 %collective-permute-done = f32[512,512]{1,0:T(8,128)S(1)} collective-permute-done((f32[512,512]{1,0:T(8,128)S(1)}, f32[512,512]{1,0:T(8,128)S(1)}, u32[]{:S(2)}, u32[]{:S(2)}) %collective-permute-start) | collective-permute-done | bytes 1048608 | tf_op jit(solution)/shard_map/ppermute | solution.py:28
  230.4 1.4 dynamic-slice_add_fusion
  231.9 2.8 collective-permute-start.1
  234.7 10.7 %collective-permute-done.1 = f32[256,512]{1,0:T(8,128)S(1)} collective-permute-done((f32[256,512]{1,0:T(8,128)S(1)}, f32[256,512]{1,0:T(8,128)S(1)}, u32[]{:S(2)}, u32[]{:S(2)}) %collective-permute-start.1) | collective-permute-done | bytes 524320 | tf_op jit(solution)/shard_map/ppermute | solution.py:28
  245.5 1.3 collective-permute-start.2
  246.8 4.0 %collective-permute-done.2 = f32[128,512]{1,0:T(8,128)S(1)} collective-permute-done((f32[128,512]{1,0:T(8,128)S(1)}, f32[128,512]{1,0:T(8,128)S(1)}, u32[]{:S(2)}, u32[]{:S(2)}) %collective-permute-start.2) | collective-permute-done | bytes 262176 | tf_op jit(solution)/shard_map/ppermute | solution.py:28
  251.9 3.6 collective-permute-start.3
  258.0 6.3 %collective-permute-done.4 = f32[128,512]{1,0:T(8,128)S(1)} collective-permute-done((f32[128,512]{1,0:T(8,128)S(1)}, f32[128,512]{1,0:T(8,128)S(1)}, u32[]{:S(2)}, u32[]{:S(2)}) %collective-permute-start.4) | collective-permute-done | bytes 262176 | tf_op jit(solution)/shard_map/ppermute | solution.py:72
  264.2 1.8 multiply_subtract_fusion
  266.0 1.3 collective-permute-start.5
  267.3 1.9 collective-permute-done.5
  269.2 2.8 collective-permute-start.6
  272.1 2.6 collective-permute-done.6
  274.8 2.8 collective-permute-start.7
  277.5 4.0 %collective-permute-done.7 = bf16[512,256]{1,0:T(8,128)(2,1)S(1)} collective-permute-done((bf16[512,256]{1,0:T(8,128)(2,1)S(1)}, bf16[512,256]{1,0:T(8,128)(2,1)S(1)}, u32[]{:S(2)}, u32[]{:S(2)}) %collective-permute-start.7) | collective-permute-done | bytes 262176 | tf_op jit(solution)/shard_map/ppermute | solution.py:39
  282.6 57.4 %all-gather.2.cloned.1.call-done = bf16[8192,256]{1,0:T(8,128)(2,1)} async-done(((bf16[1024,256]{1,0:T(8,128)(2,1)}), bf16[8192,256]{1,0:T(8,128)(2,1)}) %all-gather.2.cloned.1.call-update) | async-done | bytes 4194320 | tf_op jit(solution)/shard_map/all_gather | solution.py:82
  340.9 7.1 %collective-permute-done.8 = bf16[8192,256]{1,0:T(8,128)(2,1)} collective-permute-done((bf16[8192,256]{1,0:T(8,128)(2,1)}, bf16[8192,256]{1,0:T(8,128)(2,1)}, u32[]{:S(2)}, u32[]{:S(2)}) %collective-permute-start.8) | collective-permute-done | bytes 4194336 | tf_op jit(solution)/shard_map/ppermute | solution.py:83
  348.0 4.8 %fusion.1 = bf16[256,256]{1,0:T(8,128)(2,1)S(1)} fusion(bf16[8192,256]{1,0:T(8,128)(2,1)} %collective-permute-done.8, bf16[256,8192]{0,1:T(8,128)(2,1)} %bitcast.34), kind=kOutput, calls=%fused_computation.3 | convolution fusion | flops 1073872896 | bytes 8519680 | tf_op jit(solution)/shard_map/dot_general | solution.py:85
  (37 shorter events, 9.3 us)
Async XLA Ops:
  7.2 10.9 %copy-start = (bf16[256,512]{1,0:T(8,128)(2,1)S(1)}, bf16[256,512]{1,0:T(8,128)(2,1)}, u32[]{:S(2)}) copy-start(bf16[256,512]{1,0:T(8,128)(2,1)} %param.8) | copy-start | bytes 786436
  7.2 196.4 %reduce-scatter.2.cloned.1.call-start = ((), (), s32[]{:S(2)}) async-start(), calls=%async_computation.1 | async-start | bytes 18874368 | tf_op jit(solution)/shard_map/reduce_scatter | solution.py:60
  16.1 1.9 copy-start.1
  26.1 313.9 %all-gather.2.cloned.1.call-start = ((), (), s32[]{:S(2)}) async-start(), calls=%async_computation.2 | async-start | bytes 4718592 | tf_op jit(solution)/shard_map/all_gather | solution.py:82
  26.2 224.6 %copy-start.4 = (f32[128,512]{1,0:T(8,128)S(1)}, f32[128,512]{1,0:T(8,128)}, u32[]{:S(2)}) copy-start(f32[128,512]{1,0:T(8,128)} %param.9) | copy-start | bytes 786436
  26.2 224.6 %copy-start.6 = (f32[1,128,512]{2,1,0:T(8,128)S(1)}, f32[1,128,512]{2,1,0:T(8,128)}, u32[]{:S(2)}) copy-start(f32[1,128,512]{2,1,0:T(8,128)} %param.11) | copy-start | bytes 786436
  26.2 224.6 %copy-start.7 = (f32[1,128,512]{2,1,0:T(8,128)S(1)}, f32[1,128,512]{2,1,0:T(8,128)}, u32[]{:S(2)}) copy-start(f32[1,128,512]{2,1,0:T(8,128)} %param.13) | copy-start | bytes 786436
  26.2 224.6 %copy-start.8 = (f32[1,128,512]{2,1,0:T(8,128)S(1)}, f32[1,128,512]{2,1,0:T(8,128)}, u32[]{:S(2)}) copy-start(f32[1,128,512]{2,1,0:T(8,128)} %param.12) | copy-start | bytes 786436
  204.9 25.6 %collective-permute-start = (f32[512,512]{1,0:T(8,128)S(1)}, f32[512,512]{1,0:T(8,128)S(1)}, u32[]{:S(2)}, u32[]{:S(2)}) collective-permute-start(f32[512,512]{1,0:T(8,128)S(1)} %constant_dynamic-slice_fusion.2), channel_id=1, source_target_pairs={{0,32},{32,0},{1,33},{33,1},{2,34},{34,2},{3,35},{35,3},{4,36},{36... | collective-permute-start | bytes 3145736 | tf_op jit(solution)/shard_map/ppermute | solution.py:28
  231.9 13.5 %collective-permute-start.1 = (f32[256,512]{1,0:T(8,128)S(1)}, f32[256,512]{1,0:T(8,128)S(1)}, u32[]{:S(2)}, u32[]{:S(2)}) collective-permute-start(f32[256,512]{1,0:T(8,128)S(1)} %constant_dynamic-slice_fusion.1), channel_id=1, source_target_pairs={{0,2},{1,3},{2,0},{3,1},{4,6},{5,7},{6,4},{7,5},{8,10},{9,11},{10,... | collective-permute-start | bytes 1572872 | tf_op jit(solution)/shard_map/ppermute | solution.py:28
  245.5 5.3 %collective-permute-start.2 = (f32[128,512]{1,0:T(8,128)S(1)}, f32[128,512]{1,0:T(8,128)S(1)}, u32[]{:S(2)}, u32[]{:S(2)}) collective-permute-start(f32[128,512]{1,0:T(8,128)S(1)} %constant_dynamic-slice_fusion), channel_id=1, source_target_pairs={{0,1},{1,0},{2,3},{3,2},{4,5},{5,4},{6,7},{7,6},{8,9},{9,8},{10,11... | collective-permute-start | bytes 786440 | tf_op jit(solution)/shard_map/ppermute | solution.py:28
  251.9 4.8 %collective-permute-start.3 = (f32[128,512]{1,0:T(8,128)S(1)}, f32[128,512]{1,0:T(8,128)S(1)}, u32[]{:S(2)}, u32[]{:S(2)}) collective-permute-start(f32[128,512]{1,0:T(8,128)S(1)} %get-tuple-element.22), channel_id=1, source_target_pairs={{0,64},{64,0},{128,192},{192,128},{1,65},{65,1},{129,193},{193,129... | collective-permute-start | bytes 786440 | tf_op jit(solution)/shard_map/ppermute | solution.py:71
  256.7 7.6 %collective-permute-start.4 = (f32[128,512]{1,0:T(8,128)S(1)}, f32[128,512]{1,0:T(8,128)S(1)}, u32[]{:S(2)}, u32[]{:S(2)}) collective-permute-start(f32[128,512]{1,0:T(8,128)S(1)} %add.100), channel_id=1, source_target_pairs={{0,128},{64,192},{128,0},{192,64},{1,129},{65,193},{129,1},{193,65... | collective-permute-start | bytes 786440 | tf_op jit(solution)/shard_map/ppermute | solution.py:72
  266.0 86.8 %copy-start.5 = (f32[128,512]{1,0:T(8,128)}, f32[128,512]{1,0:T(8,128)S(1)}, u32[]{:S(2)}) copy-start(f32[128,512]{1,0:T(8,128)S(1)} %get-tuple-element.20) | copy-start | bytes 786436
  266.0 3.2 collective-permute-start.5
  269.2 5.4 %collective-permute-start.6 = (bf16[256,256]{1,0:T(8,128)(2,1)S(1)}, bf16[256,256]{1,0:T(8,128)(2,1)S(1)}, u32[]{:S(2)}, u32[]{:S(2)}) collective-permute-start(bf16[256,256]{1,0:T(8,128)(2,1)S(1)} %maximum_select_fusion.2), channel_id=1, source_target_pairs={{0,2},{1,3},{2,0},{3,1},{4,6},{5,7},{6,4},{7,5},{8,10},{9,11},{10,... | collective-permute-start | bytes 393224 | tf_op jit(solution)/shard_map/ppermute | solution.py:39
  274.8 6.8 %collective-permute-start.7 = (bf16[512,256]{1,0:T(8,128)(2,1)S(1)}, bf16[512,256]{1,0:T(8,128)(2,1)S(1)}, u32[]{:S(2)}, u32[]{:S(2)}) collective-permute-start(bf16[512,256]{1,0:T(8,128)(2,1)S(1)} %maximum_select_fusion.1), channel_id=1, source_target_pairs={{0,32},{32,0},{1,33},{33,1},{2,34},{34,2},{3,35},{35,3},{4,36},{36... | collective-permute-start | bytes 786440 | tf_op jit(solution)/shard_map/ppermute | solution.py:39
  340.0 8.0 %collective-permute-start.8 = (bf16[8192,256]{1,0:T(8,128)(2,1)}, bf16[8192,256]{1,0:T(8,128)(2,1)}, u32[]{:S(2)}, u32[]{:S(2)}) collective-permute-start(bf16[8192,256]{1,0:T(8,128)(2,1)} %all-gather.2.cloned.1.call-done), channel_id=1, source_target_pairs={{0,64},{64,0},{128,192},{192,128},{1,65},{65,1},{129,193},{193,129... | collective-permute-start | bytes 12582920 | tf_op jit(solution)/shard_map/ppermute | solution.py:83
  340.8 11.9 %copy-start.2 = (bf16[256,8,2,512]{0,3,2,1:T(8,128)(2,1)S(1)}, bf16[256,8,2,512]{0,3,2,1:T(8,128)(2,1)}, u32[]{:S(2)}) copy-start(bf16[256,8,2,512]{0,3,2,1:T(8,128)(2,1)} %copy-done.1) | copy-start | bytes 12582916
  340.8 11.9 %copy-start.3 = (bf16[8192,256]{1,0:T(8,128)(2,1)S(1)}, bf16[8192,256]{1,0:T(8,128)(2,1)}, u32[]{:S(2)}) copy-start(bf16[8192,256]{1,0:T(8,128)(2,1)} %all-gather.2.cloned.1.call-done) | copy-start | bytes 12582916
Sparse Core Ops, SparseCore 0:
  26.2 177.2 reduce-scatter.1
  282.7 57.2 all-gather.1

commit v4 on v3

--- a/solution.py
+++ b/solution.py
@@ -14,6 +14,23 @@
 decay_rate = 0.1
 outer_rate = 0.7
 nesterov = 0.9
+
+
+def ring_scatter(x, axis):
+    n = lax.axis_size(axis)
+    me = lax.axis_index(axis)
+    chunk = x.shape[0] // n
+    h = x.shape[1] // 2
+    parts = []
+    for sign, cols in ((1, slice(0, h)), (-1, slice(h, None))):
+        data = x[:, cols]
+        perm = [(i, (i + sign) % n) for i in range(n)]
+        pick = lambda k: lax.dynamic_slice_in_dim(data, (k % n) * chunk, chunk, axis=0)
+        acc = pick(me - sign + n)
+        for s in range(n - 1):
+            acc = lax.ppermute(acc, axis, perm) + pick(me - sign * (2 + s) + 2 * n)
+        parts.append(acc)
+    return jnp.concatenate(parts, axis=1)
 
 
 def halving_scatter(x, axis):
@@ -49,17 +66,20 @@
     scale = (acts.shape[0] * fsdp_count) ** (-0.5)
     xh_n, z_n, y_n = (lax.axis_size(a) for a in ("xh", "z", "y"))
     tokens = acts.shape[0]
-    acts_perm = (
-        acts.reshape(tokens, xh_n, z_n, D // (xh_n * z_n))
-        .transpose(0, 2, 1, 3)
-        .reshape(tokens, D)
-    )
-    partial = lax.dot_general(
-        acts_perm, cotangent, (((0,), (0,)), ((), ())), preferred_element_type=jnp.float32
-    )
-    grad = lax.psum_scatter(partial, "z", scatter_dimension=0, tiled=True)
-    grad = halving_scatter(grad, "xh")
-    grad = halving_scatter(grad, "y")
+    blocks = acts.reshape(tokens, xh_n, z_n, y_n, D // (xh_n * z_n * y_n))
+    acts_perm = blocks.transpose(0, 2, 1, 3, 4).reshape(tokens, D)
+    acts_yfirst = blocks.transpose(0, 3, 2, 1, 4).reshape(tokens, D)
+    cols = cotangent.shape[1] // 2
+    dims = (((0,), (0,)), ((), ()))
+    part_z = lax.dot_general(acts_perm, cotangent[:, :cols], dims, preferred_element_type=jnp.float32)
+    part_y = lax.dot_general(acts_yfirst, cotangent[:, cols:], dims, preferred_element_type=jnp.float32)
+    grad_z = lax.psum_scatter(part_z, "z", scatter_dimension=0, tiled=True)
+    grad_y = ring_scatter(part_y, "y")
+    grad_z = halving_scatter(grad_z, "xh")
+    grad_z = halving_scatter(grad_z, "y")
+    grad_y = lax.psum_scatter(grad_y, "z", scatter_dimension=0, tiled=True)
+    grad_y = halving_scatter(grad_y, "xh")
+    grad = jnp.concatenate([grad_z, grad_y], axis=1)
     grad = grad * scale
     drift = island_drift[0]
     first = beta_one * moment1[0] + (1.0 - beta_one) * grad

time: 362 us -> 282 us (0.78)
  waiting for transfers between devices: 295 us -> 175 us
  starting transfers between devices: 19.6 us -> 37.1 us
  local copies, waits for them, and re-layouts: 13.1 us -> 24.3 us
  other arithmetic: 5.48 us -> 16.1 us
    reduce_scatter x1 -> x2, waiting for transfers between devices: 177 us -> 22.2 us  [the longest x1 21.3 us: per_device(): grad_y = lax.psum_scatter(grad_y, 'z', scatter_dimension=0, tiled=True)]
    ppermute x0 -> x6, waiting for transfers between devices: none -> 61.8 us  [ring_scatter(): acc = lax.ppermute(acc, axis, perm) + pick(me - sign * (2 + s) + 2 * n)]
    ppermute x3 -> x4, waiting for transfers between devices: 37.5 us -> 11.4 us  [halving_scatter(): recv = lax.ppermute(send, axis, [(i, i ^ bit) for i in range(n)])]
    ppermute x0 -> x6, starting transfers between devices: none -> 11 us  [ring_scatter(): acc = lax.ppermute(acc, axis, perm) + pick(me - sign * (2 + s) + 2 * n)]
    add x0 -> x7, other arithmetic: none -> 10.3 us  [the longest x6 9.4 us: ring_scatter(): acc = lax.ppermute(acc, axis, perm) + pick(me - sign * (2 + s) + 2 * n)]
    ppermute x3 -> x4, starting transfers between devices: 6.89 us -> 11.7 us  [halving_scatter(): recv = lax.ppermute(send, axis, [(i, i ^ bit) for i in range(n)])]
    transpose x1 -> x2, local copies, waits for them, and re-layouts: 2.46 us -> 7.15 us  [the longest x1 4.64 us: per_device(): acts_yfirst = blocks.transpose(0, 3, 2, 1, 4).reshape(tokens, D)]
    unnamed x20 -> x24, local copies, waits for them, and re-layouts: 9.23 us -> 11.2 us
  transfers between devices with their start and end apart: 11 -> 19, of which waited for: 11 -> 16; matrix products, arithmetic and copies ran while one was open for 0% -> 10% of each run, Pallas kernels for 0% -> 0%
where the time goes in v4:
time: 282 us; the launch traced here: 281 us
  waiting for transfers between devices  175 us (62%)
  starting transfers between devices  37.1 us (13%)
  local copies, waits for them, and re-layouts  24.3 us (9%)
  other arithmetic  16.1 us (6%)
  between operations  14.1 us (5%)
  matrix products  14 us (5%)
    ppermute x6, waiting for transfers between devices, ring_scatter(): acc = lax.ppermute(acc, axis, perm) + pick(me - sign * (2 + s) + 2 * n)  61.8 us
    all_gather x1, waiting for transfers between devices, per_device(): own_full = lax.all_gather(own_full, 'z', axis=0, tiled=True)  56.6 us
    reduce_scatter x1, waiting for transfers between devices, per_device(): grad_y = lax.psum_scatter(grad_y, 'z', scatter_dimension=0, tiled=True)  21.3 us
    ppermute x4, starting transfers between devices, halving_scatter(): recv = lax.ppermute(send, axis, [(i, i ^ bit) for i in range(n)])  11.7 us
    ppermute x4, waiting for transfers between devices, halving_scatter(): recv = lax.ppermute(send, axis, [(i, i ^ bit) for i in range(n)])  11.4 us
    unnamed x24, local copies, waits for them, and re-layouts  11.2 us
    ppermute x6, starting transfers between devices, ring_scatter(): acc = lax.ppermute(acc, axis, perm) + pick(me - sign * (2 + s) + 2 * n)  11 us
    add x6, other arithmetic, ring_scatter(): acc = lax.ppermute(acc, axis, perm) + pick(me - sign * (2 + s) + 2 * n)  9.4 us
  transfers between devices with their start and end apart: 19, of which 16 were waited for; matrix products, arithmetic and copies ran while one was open for 10% of the time, Pallas kernels for 0%

profile of v4, /device:TPU:1, one launch (start us, length us, event | category | flops | bytes accessed | tf_op | source)
XLA Modules:
  0.0 281.0 jit_solution(12406346100616569511)
XLA Ops:
  7.2 6.4 %copy.19 = bf16[256,8192]{0,1:T(8,128)(2,1)} copy(bf16[256,8192]{1,0:T(8,128)(2,1)} %param.7) | data formatting | bytes 8388608 | tf_op args[0]
  18.1 4.5 %fusion.11 = f32[8192,256]{1,0:T(8,128)} fusion(bf16[256,8192]{0,1:T(8,128)(2,1)S(1)} %bitcast.44, bf16[256,512]{1,0:T(8,128)(2,1)S(1)} %copy-done.8), kind=kOutput, calls=%fused_computation.41 | convolution fusion | flops 1073741824 | bytes 12713984 | tf_op jit(solution)/shard_map/dot_general | solution.py:74
  22.7 4.6 %copy.21 = bf16[256,4,8,2,128]{0,4,3,2,1:T(8,128)(2,1)} copy(bf16[256,4,8,2,128]{0,4,1,2,3:T(8,128)(2,1)} %bitcast.48) | data formatting | bytes 8388608 | tf_op jit(solution)/shard_map/transpose | solution.py:71
  27.4 3.4 %fusion.9 = f32[8192,256]{1,0:T(8,128)S(1)} fusion(bf16[256,8192]{0,1:T(8,128)(2,1)} %bitcast.49, bf16[256,512]{1,0:T(8,128)(2,1)S(1)} %copy-done.8), kind=kOutput, calls=%fused_computation.38 | convolution fusion | flops 1073741824 | bytes 12713984 | tf_op jit(solution)/shard_map/dot_general | solution.py:75
  35.3 3.6 %collective-permute-start.6 = (f32[2048,128]{1,0:T(8,128)S(1)}, f32[2048,128]{1,0:T(8,128)S(1)}, u32[]{:S(2)}, u32[]{:S(2)}) collective-permute-start(f32[2048,128]{1,0:T(8,128)S(1)} %constant_dynamic-slice_fusion.1), channel_id=1, source_target_pairs={{0,3},{1,0},{2,1},{3,2},{4,7},{5,4},{6,5},{7,6},{8,11},{9,8},{10,9... | collective-permute-start | bytes 3145736 | tf_op jit(solution)/shard_map/ppermute | solution.py:31
  40.4 20.4 %collective-permute-done.6 = f32[2048,128]{1,0:T(8,128)S(1)} collective-permute-done((f32[2048,128]{1,0:T(8,128)S(1)}, f32[2048,128]{1,0:T(8,128)S(1)}, u32[]{:S(2)}, u32[]{:S(2)}) %collective-permute-start.6) | collective-permute-done | bytes 1048608 | tf_op jit(solution)/shard_map/ppermute | solution.py:31
  62.1 3.6 %collective-permute-start.7 = (f32[2048,128]{1,0:T(8,128)S(1)}, f32[2048,128]{1,0:T(8,128)}, u32[]{:S(2)}, u32[]{:S(2)}) collective-permute-start(f32[2048,128]{1,0:T(8,128)S(1)} %dynamic-slice_add_fusion.2), channel_id=1, source_target_pairs={{0,3},{1,0},{2,1},{3,2},{4,7},{5,4},{6,5},{7,6},{8,11},{9,8},{10,9... | collective-permute-start | bytes 3145736 | tf_op jit(solution)/shard_map/ppermute | solution.py:31
  67.5 19.3 %collective-permute-done.7 = f32[2048,128]{1,0:T(8,128)} collective-permute-done((f32[2048,128]{1,0:T(8,128)S(1)}, f32[2048,128]{1,0:T(8,128)}, u32[]{:S(2)}, u32[]{:S(2)}) %collective-permute-start.7) | collective-permute-done | bytes 1048608 | tf_op jit(solution)/shard_map/ppermute | solution.py:31
  88.5 3.5 %collective-permute-start.8 = (f32[2048,128]{1,0:T(8,128)S(1)}, f32[2048,128]{1,0:T(8,128)S(1)}, u32[]{:S(2)}, u32[]{:S(2)}) collective-permute-start(f32[2048,128]{1,0:T(8,128)S(1)} %dynamic-slice_add_fusion.1), channel_id=1, source_target_pairs={{0,3},{1,0},{2,1},{3,2},{4,7},{5,4},{6,5},{7,6},{8,11},{9,8},{10,9... | collective-permute-start | bytes 3145736 | tf_op jit(solution)/shard_map/ppermute | solution.py:31
  93.8 18.4 %collective-permute-done.8 = f32[2048,128]{1,0:T(8,128)S(1)} collective-permute-done((f32[2048,128]{1,0:T(8,128)S(1)}, f32[2048,128]{1,0:T(8,128)S(1)}, u32[]{:S(2)}, u32[]{:S(2)}) %collective-permute-start.8) | collective-permute-done | bytes 1048608 | tf_op jit(solution)/shard_map/ppermute | solution.py:31
  113.6 3.6 %collective-permute-done.5 = f32[2048,128]{1,0:T(8,128)} collective-permute-done((f32[2048,128]{1,0:T(8,128)S(1)}, f32[2048,128]{1,0:T(8,128)}, u32[]{:S(2)}, u32[]{:S(2)}) %collective-permute-start.5) | collective-permute-done | bytes 1048608 | tf_op jit(solution)/shard_map/ppermute | solution.py:31
  122.5 2.8 collective-permute-start
  125.3 9.7 %collective-permute-done = f32[512,256]{1,0:T(8,128)S(1)} collective-permute-done((f32[512,256]{1,0:T(8,128)S(1)}, f32[512,256]{1,0:T(8,128)S(1)}, u32[]{:S(2)}, u32[]{:S(2)}) %collective-permute-start) | collective-permute-done | bytes 524320 | tf_op jit(solution)/shard_map/ppermute | solution.py:45
  136.2 4.6 %collective-permute-start.1 = (f32[256,256]{1,0:T(8,128)S(1)}, f32[256,256]{1,0:T(8,128)S(1)}, u32[]{:S(2)}, u32[]{:S(2)}) collective-permute-start(f32[256,256]{1,0:T(8,128)S(1)} %constant_dynamic-slice_fusion.4), channel_id=1, source_target_pairs={{0,2},{1,3},{2,0},{3,1},{4,6},{5,7},{6,4},{7,5},{8,10},{9,11},{10,... | collective-permute-start | bytes 786440 | tf_op jit(solution)/shard_map/ppermute | solution.py:45
  140.8 21.3 %reduce-scatter.5.cloned.1.call-done = f32[256,256]{1,0:T(8,128)} async-done(((f32[2048,256]{1,0:T(8,128)}), f32[256,256]{1,0:T(8,128)}) %reduce-scatter.5.cloned.1.call-update) | async-done | bytes 262160 | tf_op jit(solution)/shard_map/reduce_scatter | solution.py:80
  163.0 2.8 %collective-permute-start.9 = (f32[128,256]{1,0:T(8,128)S(1)}, f32[128,256]{1,0:T(8,128)S(1)}, u32[]{:S(2)}, u32[]{:S(2)}) collective-permute-start(f32[128,256]{1,0:T(8,128)S(1)} %constant_dynamic-slice_fusion), channel_id=1, source_target_pairs={{0,32},{32,0},{1,33},{33,1},{2,34},{34,2},{3,35},{35,3},{4,36},{36... | collective-permute-start | bytes 393224 | tf_op jit(solution)/shard_map/ppermute | solution.py:45
  170.3 6.2 %collective-permute-start.10 = (f32[128,512]{1,0:T(8,128)S(1)}, f32[128,512]{1,0:T(8,128)S(1)}, u32[]{:S(2)}, u32[]{:S(2)}) collective-permute-start(f32[128,512]{1,0:T(8,128)S(1)} %fusion.7), channel_id=1, source_target_pairs={{0,64},{64,0},{128,192},{192,128},{1,65},{65,1},{129,193},{193,129... | collective-permute-start | bytes 786440 | tf_op jit(solution)/shard_map/ppermute | solution.py:91
  178.5 6.8 %collective-permute-done.11 = f32[128,512]{1,0:T(8,128)S(1)} collective-permute-done((f32[128,512]{1,0:T(8,128)S(1)}, f32[128,512]{1,0:T(8,128)S(1)}, u32[]{:S(2)}, u32[]{:S(2)}) %collective-permute-start.11) | collective-permute-done | bytes 262176 | tf_op jit(solution)/shard_map/ppermute | solution.py:92
  189.5 2.7 collective-permute-start.13
  192.2 2.7 collective-permute-done.13
  197.0 4.9 %collective-permute-done.14 = bf16[512,256]{1,0:T(8,128)(2,1)S(1)} collective-permute-done((bf16[512,256]{1,0:T(8,128)(2,1)S(1)}, bf16[512,256]{1,0:T(8,128)(2,1)S(1)}, u32[]{:S(2)}, u32[]{:S(2)}) %collective-permute-start.14) | collective-permute-done | bytes 262176 | tf_op jit(solution)/shard_map/ppermute | solution.py:56
  202.9 56.6 %all-gather.2.cloned.1.call-done = bf16[8192,256]{1,0:T(8,128)(2,1)} async-done(((bf16[1024,256]{1,0:T(8,128)(2,1)}), bf16[8192,256]{1,0:T(8,128)(2,1)}) %all-gather.2.cloned.1.call-update) | async-done | bytes 4194320 | tf_op jit(solution)/shard_map/all_gather | solution.py:102
  261.3 6.2 %collective-permute-done.15 = bf16[8192,256]{1,0:T(8,128)(2,1)} collective-permute-done((bf16[8192,256]{1,0:T(8,128)(2,1)}, bf16[8192,256]{1,0:T(8,128)(2,1)}, u32[]{:S(2)}, u32[]{:S(2)}) %collective-permute-start.15) | collective-permute-done | bytes 4194336 | tf_op jit(solution)/shard_map/ppermute | solution.py:103
  267.5 4.8 %fusion.1 = bf16[256,256]{1,0:T(8,128)(2,1)S(1)} fusion(bf16[8192,256]{1,0:T(8,128)(2,1)} %collective-permute-done.15, bf16[256,8192]{0,1:T(8,128)(2,1)} %bitcast.45), kind=kOutput, calls=%fused_computation.4 | convolution fusion | flops 1073872896 | bytes 8519680 | tf_op jit(solution)/shard_map/dot_general | solution.py:105
  (74 shorter events, 43.2 us)
Async XLA Ops:
  7.2 114.3 %reduce-scatter.3.cloned.1.call-start = ((), (), s32[]{:S(2)}) async-start(), calls=%async_computation.2 | async-start | bytes 9437184 | tf_op jit(solution)/shard_map/reduce_scatter | solution.py:76
  22.7 139.4 %reduce-scatter.5.cloned.1.call-start = ((), (), s32[]{:S(2)}) async-start(), calls=%async_computation.3 | async-start | bytes 2359296 | tf_op jit(solution)/shard_map/reduce_scatter | solution.py:80
  35.3 25.5 %collective-permute-start.6 = (f32[2048,128]{1,0:T(8,128)S(1)}, f32[2048,128]{1,0:T(8,128)S(1)}, u32[]{:S(2)}, u32[]{:S(2)}) collective-permute-start(f32[2048,128]{1,0:T(8,128)S(1)} %constant_dynamic-slice_fusion.1), channel_id=1, source_target_pairs={{0,3},{1,0},{2,1},{3,2},{4,7},{5,4},{6,5},{7,6},{8,11},{9,8},{10,9... | collective-permute-start | bytes 3145736 | tf_op jit(solution)/shard_map/ppermute | solution.py:31
  40.2 25.5 %collective-permute-start.3 = (f32[2048,128]{1,0:T(8,128)S(1)}, f32[2048,128]{1,0:T(8,128)}, u32[]{:S(2)}, u32[]{:S(2)}) collective-permute-start(f32[2048,128]{1,0:T(8,128)S(1)} %constant_dynamic-slice_fusion.2), channel_id=1, source_target_pairs={{0,1},{1,2},{2,3},{3,0},{4,5},{5,6},{6,7},{7,4},{8,9},{9,10},{10,1... | collective-permute-start | bytes 3145736 | tf_op jit(solution)/shard_map/ppermute | solution.py:31
  62.1 24.7 %collective-permute-start.7 = (f32[2048,128]{1,0:T(8,128)S(1)}, f32[2048,128]{1,0:T(8,128)}, u32[]{:S(2)}, u32[]{:S(2)}) collective-permute-start(f32[2048,128]{1,0:T(8,128)S(1)} %dynamic-slice_add_fusion.2), channel_id=1, source_target_pairs={{0,3},{1,0},{2,1},{3,2},{4,7},{5,4},{6,5},{7,6},{8,11},{9,8},{10,9... | collective-permute-start | bytes 3145736 | tf_op jit(solution)/shard_map/ppermute | solution.py:31
  67.4 24.7 %collective-permute-start.4 = (f32[2048,128]{1,0:T(8,128)S(1)}, f32[2048,128]{1,0:T(8,128)}, u32[]{:S(2)}, u32[]{:S(2)}) collective-permute-start(f32[2048,128]{1,0:T(8,128)S(1)} %dynamic-slice_add_fusion.5), channel_id=1, source_target_pairs={{0,1},{1,2},{2,3},{3,0},{4,5},{5,6},{6,7},{7,4},{8,9},{9,10},{10,1... | collective-permute-start | bytes 3145736 | tf_op jit(solution)/shard_map/ppermute | solution.py:31
  88.5 23.7 %collective-permute-start.8 = (f32[2048,128]{1,0:T(8,128)S(1)}, f32[2048,128]{1,0:T(8,128)S(1)}, u32[]{:S(2)}, u32[]{:S(2)}) collective-permute-start(f32[2048,128]{1,0:T(8,128)S(1)} %dynamic-slice_add_fusion.1), channel_id=1, source_target_pairs={{0,3},{1,0},{2,1},{3,2},{4,7},{5,4},{6,5},{7,6},{8,11},{9,8},{10,9... | collective-permute-start | bytes 3145736 | tf_op jit(solution)/shard_map/ppermute | solution.py:31
  93.7 23.6 %collective-permute-start.5 = (f32[2048,128]{1,0:T(8,128)S(1)}, f32[2048,128]{1,0:T(8,128)}, u32[]{:S(2)}, u32[]{:S(2)}) collective-permute-start(f32[2048,128]{1,0:T(8,128)S(1)} %dynamic-slice_add_fusion.4), channel_id=1, source_target_pairs={{0,1},{1,2},{2,3},{3,0},{4,5},{5,6},{6,7},{7,4},{8,9},{9,10},{10,1... | collective-permute-start | bytes 3145736 | tf_op jit(solution)/shard_map/ppermute | solution.py:31
  120.4 49.6 %copy-start.5 = (f32[1,128,512]{2,1,0:T(8,128)S(1)}, f32[1,128,512]{2,1,0:T(8,128)}, u32[]{:S(2)}) copy-start(f32[1,128,512]{2,1,0:T(8,128)} %param.12) | copy-start | bytes 786436
  120.4 49.6 %copy-start.6 = (f32[128,512]{1,0:T(8,128)S(1)}, f32[128,512]{1,0:T(8,128)}, u32[]{:S(2)}) copy-start(f32[128,512]{1,0:T(8,128)} %param.9) | copy-start | bytes 786436
  120.4 49.6 %copy-start.9 = (f32[1,128,512]{2,1,0:T(8,128)S(1)}, f32[1,128,512]{2,1,0:T(8,128)}, u32[]{:S(2)}) copy-start(f32[1,128,512]{2,1,0:T(8,128)} %param.11) | copy-start | bytes 786436
  120.4 64.9 %copy-start.10 = (f32[128,512]{1,0:T(8,128)S(1)}, f32[128,512]{1,0:T(8,128)}, u32[]{:S(2)}) copy-start(f32[128,512]{1,0:T(8,128)} %param.10) | copy-start | bytes 786436
  120.4 139.1 %all-gather.2.cloned.1.call-start = ((), (), s32[]{:S(2)}) async-start(), calls=%async_computation.4 | async-start | bytes 4718592 | tf_op jit(solution)/shard_map/all_gather | solution.py:102
  122.5 12.5 %collective-permute-start = (f32[512,256]{1,0:T(8,128)S(1)}, f32[512,256]{1,0:T(8,128)S(1)}, u32[]{:S(2)}, u32[]{:S(2)}) collective-permute-start(f32[512,256]{1,0:T(8,128)S(1)} %constant_dynamic-slice_fusion.5), channel_id=1, source_target_pairs={{0,32},{32,0},{1,33},{33,1},{2,34},{34,2},{3,35},{35,3},{4,36},{36... | collective-permute-start | bytes 1572872 | tf_op jit(solution)/shard_map/ppermute | solution.py:45
  136.2 29.6 %collective-permute-start.1 = (f32[256,256]{1,0:T(8,128)S(1)}, f32[256,256]{1,0:T(8,128)S(1)}, u32[]{:S(2)}, u32[]{:S(2)}) collective-permute-start(f32[256,256]{1,0:T(8,128)S(1)} %constant_dynamic-slice_fusion.4), channel_id=1, source_target_pairs={{0,2},{1,3},{2,0},{3,1},{4,6},{5,7},{6,4},{7,5},{8,10},{9,11},{10,... | collective-permute-start | bytes 786440 | tf_op jit(solution)/shard_map/ppermute | solution.py:45
  163.0 5.4 %collective-permute-start.9 = (f32[128,256]{1,0:T(8,128)S(1)}, f32[128,256]{1,0:T(8,128)S(1)}, u32[]{:S(2)}, u32[]{:S(2)}) collective-permute-start(f32[128,256]{1,0:T(8,128)S(1)} %constant_dynamic-slice_fusion), channel_id=1, source_target_pairs={{0,32},{32,0},{1,33},{33,1},{2,34},{34,2},{3,35},{35,3},{4,36},{36... | collective-permute-start | bytes 393224 | tf_op jit(solution)/shard_map/ppermute | solution.py:45
  165.9 4.1 %collective-permute-start.2 = (f32[128,256]{1,0:T(8,128)S(1)}, f32[128,256]{1,0:T(8,128)S(1)}, u32[]{:S(2)}, u32[]{:S(2)}) collective-permute-start(f32[128,256]{1,0:T(8,128)S(1)} %constant_dynamic-slice_fusion.3), channel_id=1, source_target_pairs={{0,1},{1,0},{2,3},{3,2},{4,5},{5,4},{6,7},{7,6},{8,9},{9,8},{10,11... | collective-permute-start | bytes 393224 | tf_op jit(solution)/shard_map/ppermute | solution.py:45
  170.3 7.4 %collective-permute-start.10 = (f32[128,512]{1,0:T(8,128)S(1)}, f32[128,512]{1,0:T(8,128)S(1)}, u32[]{:S(2)}, u32[]{:S(2)}) collective-permute-start(f32[128,512]{1,0:T(8,128)S(1)} %fusion.7), channel_id=1, source_target_pairs={{0,64},{64,0},{128,192},{192,128},{1,65},{65,1},{129,193},{193,129... | collective-permute-start | bytes 786440 | tf_op jit(solution)/shard_map/ppermute | solution.py:91
  177.7 7.6 %collective-permute-start.11 = (f32[128,512]{1,0:T(8,128)S(1)}, f32[128,512]{1,0:T(8,128)S(1)}, u32[]{:S(2)}, u32[]{:S(2)}) collective-permute-start(f32[128,512]{1,0:T(8,128)S(1)} %add.256), channel_id=1, source_target_pairs={{0,128},{64,192},{128,0},{192,64},{1,129},{65,193},{129,1},{193,65... | collective-permute-start | bytes 786440 | tf_op jit(solution)/shard_map/ppermute | solution.py:92
  186.1 86.2 %copy-start.7 = (f32[128,512]{1,0:T(8,128)}, f32[128,512]{1,0:T(8,128)S(1)}, u32[]{:S(2)}) copy-start(f32[128,512]{1,0:T(8,128)S(1)} %get-tuple-element.20) | copy-start | bytes 786436
  186.1 3.4 %collective-permute-start.12 = (bf16[128,256]{1,0:T(8,128)(2,1)S(1)}, bf16[128,256]{1,0:T(8,128)(2,1)S(1)}, u32[]{:S(2)}, u32[]{:S(2)}) collective-permute-start(bf16[128,256]{1,0:T(8,128)(2,1)S(1)} %dynamic-slice_convert_fusion), channel_id=1, source_target_pairs={{0,1},{1,0},{2,3},{3,2},{4,5},{5,4},{6,7},{7,6},{8,9},{9,8},{10,11... | collective-permute-start | bytes 196616 | tf_op jit(solution)/shard_map/ppermute | solution.py:56
  189.5 5.4 %collective-permute-start.13 = (bf16[256,256]{1,0:T(8,128)(2,1)S(1)}, bf16[256,256]{1,0:T(8,128)(2,1)S(1)}, u32[]{:S(2)}, u32[]{:S(2)}) collective-permute-start(bf16[256,256]{1,0:T(8,128)(2,1)S(1)} %maximum_select_fusion.2), channel_id=1, source_target_pairs={{0,2},{1,3},{2,0},{3,1},{4,6},{5,7},{6,4},{7,5},{8,10},{9,11},{10,... | collective-permute-start | bytes 393224 | tf_op jit(solution)/shard_map/ppermute | solution.py:56
  195.0 6.8 %collective-permute-start.14 = (bf16[512,256]{1,0:T(8,128)(2,1)S(1)}, bf16[512,256]{1,0:T(8,128)(2,1)S(1)}, u32[]{:S(2)}, u32[]{:S(2)}) collective-permute-start(bf16[512,256]{1,0:T(8,128)(2,1)S(1)} %maximum_select_fusion.1), channel_id=1, source_target_pairs={{0,32},{32,0},{1,33},{33,1},{2,34},{34,2},{3,35},{35,3},{4,36},{36... | collective-permute-start | bytes 786440 | tf_op jit(solution)/shard_map/ppermute | solution.py:56
  259.6 8.0 %collective-permute-start.15 = (bf16[8192,256]{1,0:T(8,128)(2,1)}, bf16[8192,256]{1,0:T(8,128)(2,1)}, u32[]{:S(2)}, u32[]{:S(2)}) collective-permute-start(bf16[8192,256]{1,0:T(8,128)(2,1)} %all-gather.2.cloned.1.call-done), channel_id=1, source_target_pairs={{0,64},{64,0},{128,192},{192,128},{1,65},{65,1},{129,193},{193,129... | collective-permute-start | bytes 12582920 | tf_op jit(solution)/shard_map/ppermute | solution.py:103
  (6 other events, 80.1 us)
Sparse Core Ops, SparseCore 0:
  22.8 98.6 reduce-scatter.2
  124.0 38.0 reduce-scatter.4
  203.0 56.4 all-gather.1

commit v5 on v4

--- a/solution.py
+++ b/solution.py
@@ -97,12 +97,19 @@
     core = lax.axis_index("island") % 2
     half = weights.shape[1] // 2
     own = lax.dynamic_slice_in_dim(weights, core * half, half, axis=1)
-    own_full = doubling_gather(own, "y")
-    own_full = doubling_gather(own_full, "xh")
-    own_full = lax.all_gather(own_full, "z", axis=0, tiled=True)
-    other_full = lax.ppermute(own_full, "island", pair_core)
-    keys_own = jnp.dot(acts_perm, own_full, preferred_element_type=jnp.float32)
-    keys_other = jnp.dot(acts_perm, other_full, preferred_element_type=jnp.float32)
+    quarter = half // 2
+    full_p = doubling_gather(own[:, :quarter], "y")
+    full_p = doubling_gather(full_p, "xh")
+    full_p = lax.all_gather(full_p, "z", axis=0, tiled=True)
+    acts_q = blocks.transpose(0, 1, 3, 2, 4).reshape(tokens, D)
+    full_q = lax.all_gather(own[:, quarter:], "z", axis=0, tiled=True)
+    full_q = doubling_gather(full_q, "y")
+    full_q = doubling_gather(full_q, "xh")
+    other_p = lax.ppermute(full_p, "island", pair_core)
+    other_q = lax.ppermute(full_q, "island", pair_core)
+    dot = lambda a, w: jnp.dot(a, w, preferred_element_type=jnp.float32)
+    keys_own = jnp.concatenate([dot(acts_perm, full_p), dot(acts_q, full_q)], axis=1)
+    keys_other = jnp.concatenate([dot(acts_perm, other_p), dot(acts_q, other_q)], axis=1)
     keys_own = (keys_own * D ** (-0.5)).astype(jnp.bfloat16)
     keys_other = (keys_other * D ** (-0.5)).astype(jnp.bfloat16)
     is_first = core == 0

time: 282 us -> 285 us (1.011)
  waiting for transfers between devices: 175 us -> 134 us
  starting transfers between devices: 37.1 us -> 57 us
  blocking collectives: 0 us -> 18.7 us
  local copies, waits for them, and re-layouts: 24.3 us -> 28 us
    all_gather x1, waiting for transfers between devices: 56.6 us -> 0.01 us  [per_device(): full_p = lax.all_gather(full_p, 'z', axis=0, tiled=True)]
    ppermute x3 -> x6, waiting for transfers between devices: 9.25 us -> 30.3 us  [doubling_gather(): recv = lax.ppermute(x, axis, [(i, i ^ bit) for i in range(n)])]
    all_gather x0 -> x1, blocking collectives: none -> 18.7 us  [per_device(): full_q = lax.all_gather(own[:, quarter:], 'z', axis=0, tiled=True)]
    ppermute x1 -> x2, starting transfers between devices: 0.84 us -> 16.8 us  [the longest x1 14 us: per_device(): other_q = lax.ppermute(full_q, 'island', pair_core)]
    ppermute x1 -> x2, waiting for transfers between devices: 6.24 us -> 0.01 us  [the longest x1 0.01 us: per_device(): other_q = lax.ppermute(full_q, 'island', pair_core)]
    ppermute x3 -> x6, starting transfers between devices: 6.33 us -> 10.5 us  [doubling_gather(): recv = lax.ppermute(x, axis, [(i, i ^ bit) for i in range(n)])]
    dot_general x2 -> x4, matrix products: 6.06 us -> 6.85 us  [per_device(): dot = lambda a, w: jnp.dot(a, w, preferred_element_type=jnp.float32)]
  transfers between devices with their start and end apart: 19 -> 23, of which waited for: 16 -> 16; matrix products, arithmetic and copies ran while one was open for 10% -> 13% of each run, Pallas kernels for 0% -> 0%
where the time goes in v5:
time: 285 us; the launch traced here: 284 us
  waiting for transfers between devices  134 us (47%)
  starting transfers between devices  57 us (20%)
  local copies, waits for them, and re-layouts  28 us (10%)
  blocking collectives  18.7 us (7%)
  other arithmetic  16.9 us (6%)
  matrix products  14.8 us (5%)
  between operations  14.1 us (5%)
    ppermute x6, waiting for transfers between devices, ring_scatter(): acc = lax.ppermute(acc, axis, perm) + pick(me - sign * (2 + s) + 2 * n)  61.8 us
    ppermute x6, waiting for transfers between devices, doubling_gather(): recv = lax.ppermute(x, axis, [(i, i ^ bit) for i in range(n)])  30.3 us
    reduce_scatter x1, waiting for transfers between devices, per_device(): grad_y = lax.psum_scatter(grad_y, 'z', scatter_dimension=0, tiled=True)  21.6 us
    all_gather x1, blocking collectives, per_device(): full_q = lax.all_gather(own[:, quarter:], 'z', axis=0, tiled=True)  18.7 us
    ppermute x1, starting transfers between devices, per_device(): other_q = lax.ppermute(full_q, 'island', pair_core)  14 us
    unnamed x24, local copies, waits for them, and re-layouts  12.5 us
    ppermute x4, starting transfers between devices, halving_scatter(): recv = lax.ppermute(send, axis, [(i, i ^ bit) for i in range(n)])  11.5 us
    ppermute x4, waiting for transfers between devices, halving_scatter(): recv = lax.ppermute(send, axis, [(i, i ^ bit) for i in range(n)])  11.4 us
  transfers between devices with their start and end apart: 23, of which 16 were waited for; matrix products, arithmetic and copies ran while one was open for 13% of the time, Pallas kernels for 0%

profile of v5, /device:TPU:1, one launch (start us, length us, event | category | flops | bytes accessed | tf_op | source)
XLA Modules:
  0.0 283.8 jit_solution(2543196815621117303)
XLA Ops:
  7.2 6.4 %copy.20 = bf16[256,8192]{0,1:T(8,128)(2,1)} copy(bf16[256,8192]{1,0:T(8,128)(2,1)} %param.7) | data formatting | bytes 8388608 | tf_op args[0]
  18.1 4.5 %fusion.11 = f32[8192,256]{1,0:T(8,128)} fusion(bf16[256,8192]{0,1:T(8,128)(2,1)S(1)} %bitcast.55, bf16[256,512]{1,0:T(8,128)(2,1)S(1)} %copy-done.8), kind=kOutput, calls=%fused_computation.45 | convolution fusion | flops 1073741824 | bytes 12713984 | tf_op jit(solution)/shard_map/dot_general | solution.py:74
  22.7 4.7 %copy.22 = bf16[256,4,8,2,128]{0,4,3,2,1:T(8,128)(2,1)} copy(bf16[256,4,8,2,128]{0,4,1,2,3:T(8,128)(2,1)} %bitcast.59) | data formatting | bytes 8388608 | tf_op jit(solution)/shard_map/transpose | solution.py:71
  27.4 3.4 %fusion.9 = f32[8192,256]{1,0:T(8,128)S(1)} fusion(bf16[256,8192]{0,1:T(8,128)(2,1)} %bitcast.63, bf16[256,512]{1,0:T(8,128)(2,1)S(1)} %copy-done.8), kind=kOutput, calls=%fused_computation.42 | convolution fusion | flops 1073741824 | bytes 12713984 | tf_op jit(solution)/shard_map/dot_general | solution.py:75
  35.4 3.6 %collective-permute-start.6 = (f32[2048,128]{1,0:T(8,128)S(1)}, f32[2048,128]{1,0:T(8,128)S(1)}, u32[]{:S(2)}, u32[]{:S(2)}) collective-permute-start(f32[2048,128]{1,0:T(8,128)S(1)} %constant_dynamic-slice_fusion.1), channel_id=1, source_target_pairs={{0,3},{1,0},{2,1},{3,2},{4,7},{5,4},{6,5},{7,6},{8,11},{9,8},{10,9... | collective-permute-start | bytes 3145736 | tf_op jit(solution)/shard_map/ppermute | solution.py:31
  40.5 20.4 %collective-permute-done.6 = f32[2048,128]{1,0:T(8,128)S(1)} collective-permute-done((f32[2048,128]{1,0:T(8,128)S(1)}, f32[2048,128]{1,0:T(8,128)S(1)}, u32[]{:S(2)}, u32[]{:S(2)}) %collective-permute-start.6) | collective-permute-done | bytes 1048608 | tf_op jit(solution)/shard_map/ppermute | solution.py:31
  62.2 3.6 %collective-permute-start.7 = (f32[2048,128]{1,0:T(8,128)S(1)}, f32[2048,128]{1,0:T(8,128)}, u32[]{:S(2)}, u32[]{:S(2)}) collective-permute-start(f32[2048,128]{1,0:T(8,128)S(1)} %dynamic-slice_add_fusion.2), channel_id=1, source_target_pairs={{0,3},{1,0},{2,1},{3,2},{4,7},{5,4},{6,5},{7,6},{8,11},{9,8},{10,9... | collective-permute-start | bytes 3145736 | tf_op jit(solution)/shard_map/ppermute | solution.py:31
  67.6 19.3 %collective-permute-done.7 = f32[2048,128]{1,0:T(8,128)} collective-permute-done((f32[2048,128]{1,0:T(8,128)S(1)}, f32[2048,128]{1,0:T(8,128)}, u32[]{:S(2)}, u32[]{:S(2)}) %collective-permute-start.7) | collective-permute-done | bytes 1048608 | tf_op jit(solution)/shard_map/ppermute | solution.py:31
  88.7 3.5 %collective-permute-start.8 = (f32[2048,128]{1,0:T(8,128)S(1)}, f32[2048,128]{1,0:T(8,128)S(1)}, u32[]{:S(2)}, u32[]{:S(2)}) collective-permute-start(f32[2048,128]{1,0:T(8,128)S(1)} %dynamic-slice_add_fusion.1), channel_id=1, source_target_pairs={{0,3},{1,0},{2,1},{3,2},{4,7},{5,4},{6,5},{7,6},{8,11},{9,8},{10,9... | collective-permute-start | bytes 3145736 | tf_op jit(solution)/shard_map/ppermute | solution.py:31
  94.0 18.4 %collective-permute-done.8 = f32[2048,128]{1,0:T(8,128)S(1)} collective-permute-done((f32[2048,128]{1,0:T(8,128)S(1)}, f32[2048,128]{1,0:T(8,128)S(1)}, u32[]{:S(2)}, u32[]{:S(2)}) %collective-permute-start.8) | collective-permute-done | bytes 1048608 | tf_op jit(solution)/shard_map/ppermute | solution.py:31
  113.8 3.7 %collective-permute-done.5 = f32[2048,128]{1,0:T(8,128)} collective-permute-done((f32[2048,128]{1,0:T(8,128)S(1)}, f32[2048,128]{1,0:T(8,128)}, u32[]{:S(2)}, u32[]{:S(2)}) %collective-permute-start.5) | collective-permute-done | bytes 1048608 | tf_op jit(solution)/shard_map/ppermute | solution.py:31
  122.5 2.8 collective-permute-start
  125.3 9.5 %collective-permute-done = f32[512,256]{1,0:T(8,128)S(1)} collective-permute-done((f32[512,256]{1,0:T(8,128)S(1)}, f32[512,256]{1,0:T(8,128)S(1)}, u32[]{:S(2)}, u32[]{:S(2)}) %collective-permute-start) | collective-permute-done | bytes 524320 | tf_op jit(solution)/shard_map/ppermute | solution.py:45
  136.0 4.8 %collective-permute-start.1 = (f32[256,256]{1,0:T(8,128)S(1)}, f32[256,256]{1,0:T(8,128)S(1)}, u32[]{:S(2)}, u32[]{:S(2)}) collective-permute-start(f32[256,256]{1,0:T(8,128)S(1)} %constant_dynamic-slice_fusion.4), channel_id=1, source_target_pairs={{0,2},{1,3},{2,0},{3,1},{4,6},{5,7},{6,4},{7,5},{8,10},{9,11},{10,... | collective-permute-start | bytes 786440 | tf_op jit(solution)/shard_map/ppermute | solution.py:45
  140.8 21.6 %reduce-scatter.5.cloned.1.call-done = f32[256,256]{1,0:T(8,128)} async-done(((f32[2048,256]{1,0:T(8,128)}), f32[256,256]{1,0:T(8,128)}) %reduce-scatter.5.cloned.1.call-update) | async-done | bytes 262160 | tf_op jit(solution)/shard_map/reduce_scatter | solution.py:80
  170.4 6.6 %collective-permute-start.10 = (f32[128,512]{1,0:T(8,128)S(1)}, f32[128,512]{1,0:T(8,128)S(1)}, u32[]{:S(2)}, u32[]{:S(2)}) collective-permute-start(f32[128,512]{1,0:T(8,128)S(1)} %fusion.7), channel_id=1, source_target_pairs={{0,64},{64,0},{128,192},{192,128},{1,65},{65,1},{129,193},{193,129... | collective-permute-start | bytes 786440 | tf_op jit(solution)/shard_map/ppermute | solution.py:91
  178.6 7.2 %collective-permute-done.11 = f32[128,512]{1,0:T(8,128)S(1)} collective-permute-done((f32[128,512]{1,0:T(8,128)S(1)}, f32[128,512]{1,0:T(8,128)S(1)}, u32[]{:S(2)}, u32[]{:S(2)}) %collective-permute-start.11) | collective-permute-done | bytes 262176 | tf_op jit(solution)/shard_map/ppermute | solution.py:92
  189.6 2.7 collective-permute-start.13
  196.2 18.7 %all_gather.7 = bf16[1024,128]{1,0:T(8,128)(2,1)S(1)} all-gather(bf16[128,128]{1,0:T(8,128)(2,1)S(1)} %get-tuple-element.29), channel_id=1, replica_groups=mesh['island'=4,'xh'=2,'z'=8,'y'=4] {'z'}, dimensions={0}, use_global_device_ids=true | all-gather | bytes 294912 | tf_op jit(solution)/shard_map/all_gather | solution.py:105
  216.9 3.6 %collective-permute-done.15 = bf16[1024,128]{1,0:T(8,128)(2,1)S(1)} collective-permute-done((bf16[1024,128]{1,0:T(8,128)(2,1)S(1)}, bf16[1024,128]{1,0:T(8,128)(2,1)S(1)}, u32[]{:S(2)}, u32[]{:S(2)}) %collective-permute-start.15) | collective-permute-done | bytes 262176 | tf_op jit(solution)/shard_map/ppermute | solution.py:56
  223.3 8.6 %collective-permute-done.16 = bf16[2048,128]{1,0:T(8,128)(2,1)S(1)} collective-permute-done((bf16[2048,128]{1,0:T(8,128)(2,1)S(1)}, bf16[2048,128]{1,0:T(8,128)(2,1)S(1)}, u32[]{:S(2)}, u32[]{:S(2)}) %collective-permute-start.16) | collective-permute-done | bytes 524320 | tf_op jit(solution)/shard_map/ppermute | solution.py:56
  233.0 14.5 %collective-permute-done.17 = bf16[4096,128]{1,0:T(8,128)(2,1)S(1)} collective-permute-done((bf16[4096,128]{1,0:T(8,128)(2,1)S(1)}, bf16[4096,128]{1,0:T(8,128)(2,1)S(1)}, u32[]{:S(2)}, u32[]{:S(2)}) %collective-permute-start.17) | collective-permute-done | bytes 1048608 | tf_op jit(solution)/shard_map/ppermute | solution.py:56
  248.0 14.0 %collective-permute-start.19 = (bf16[8192,128]{1,0:T(8,128)(2,1)S(1)}, bf16[8192,128]{1,0:T(8,128)(2,1)}, u32[]{:S(2)}, u32[]{:S(2)}) collective-permute-start(bf16[8192,128]{1,0:T(8,128)(2,1)S(1)} %maximum_select_fusion), channel_id=1, source_target_pairs={{0,64},{64,0},{128,192},{192,128},{1,65},{65,1},{129,193},{193,129... | collective-permute-start | bytes 6291464 | tf_op jit(solution)/shard_map/ppermute | solution.py:109
  262.0 2.9 %collective-permute-start.18 = (bf16[8192,128]{1,0:T(8,128)(2,1)}, bf16[8192,128]{1,0:T(8,128)(2,1)}, u32[]{:S(2)}, u32[]{:S(2)}) collective-permute-start(bf16[8192,128]{1,0:T(8,128)(2,1)} %all-gather.2.cloned.1.call-done), channel_id=1, source_target_pairs={{0,64},{64,0},{128,192},{192,128},{1,65},{65,1},{129,193},{193,129... | collective-permute-start | bytes 6291464 | tf_op jit(solution)/shard_map/ppermute | solution.py:108
  (91 shorter events, 60.6 us)
Async XLA Ops:
  7.2 114.3 %reduce-scatter.3.cloned.1.call-start = ((), (), s32[]{:S(2)}) async-start(), calls=%async_computation.2 | async-start | bytes 9437184 | tf_op jit(solution)/shard_map/reduce_scatter | solution.py:76
  22.6 139.8 %reduce-scatter.5.cloned.1.call-start = ((), (), s32[]{:S(2)}) async-start(), calls=%async_computation.3 | async-start | bytes 2359296 | tf_op jit(solution)/shard_map/reduce_scatter | solution.py:80
  35.4 25.5 %collective-permute-start.6 = (f32[2048,128]{1,0:T(8,128)S(1)}, f32[2048,128]{1,0:T(8,128)S(1)}, u32[]{:S(2)}, u32[]{:S(2)}) collective-permute-start(f32[2048,128]{1,0:T(8,128)S(1)} %constant_dynamic-slice_fusion.1), channel_id=1, source_target_pairs={{0,3},{1,0},{2,1},{3,2},{4,7},{5,4},{6,5},{7,6},{8,11},{9,8},{10,9... | collective-permute-start | bytes 3145736 | tf_op jit(solution)/shard_map/ppermute | solution.py:31
  40.3 25.5 %collective-permute-start.3 = (f32[2048,128]{1,0:T(8,128)S(1)}, f32[2048,128]{1,0:T(8,128)}, u32[]{:S(2)}, u32[]{:S(2)}) collective-permute-start(f32[2048,128]{1,0:T(8,128)S(1)} %constant_dynamic-slice_fusion.2), channel_id=1, source_target_pairs={{0,1},{1,2},{2,3},{3,0},{4,5},{5,6},{6,7},{7,4},{8,9},{9,10},{10,1... | collective-permute-start | bytes 3145736 | tf_op jit(solution)/shard_map/ppermute | solution.py:31
  62.2 24.7 %collective-permute-start.7 = (f32[2048,128]{1,0:T(8,128)S(1)}, f32[2048,128]{1,0:T(8,128)}, u32[]{:S(2)}, u32[]{:S(2)}) collective-permute-start(f32[2048,128]{1,0:T(8,128)S(1)} %dynamic-slice_add_fusion.2), channel_id=1, source_target_pairs={{0,3},{1,0},{2,1},{3,2},{4,7},{5,4},{6,5},{7,6},{8,11},{9,8},{10,9... | collective-permute-start | bytes 3145736 | tf_op jit(solution)/shard_map/ppermute | solution.py:31
  67.5 24.7 %collective-permute-start.4 = (f32[2048,128]{1,0:T(8,128)S(1)}, f32[2048,128]{1,0:T(8,128)}, u32[]{:S(2)}, u32[]{:S(2)}) collective-permute-start(f32[2048,128]{1,0:T(8,128)S(1)} %dynamic-slice_add_fusion.5), channel_id=1, source_target_pairs={{0,1},{1,2},{2,3},{3,0},{4,5},{5,6},{6,7},{7,4},{8,9},{9,10},{10,1... | collective-permute-start | bytes 3145736 | tf_op jit(solution)/shard_map/ppermute | solution.py:31
  88.7 23.7 %collective-permute-start.8 = (f32[2048,128]{1,0:T(8,128)S(1)}, f32[2048,128]{1,0:T(8,128)S(1)}, u32[]{:S(2)}, u32[]{:S(2)}) collective-permute-start(f32[2048,128]{1,0:T(8,128)S(1)} %dynamic-slice_add_fusion.1), channel_id=1, source_target_pairs={{0,3},{1,0},{2,1},{3,2},{4,7},{5,4},{6,5},{7,6},{8,11},{9,8},{10,9... | collective-permute-start | bytes 3145736 | tf_op jit(solution)/shard_map/ppermute | solution.py:31
  93.9 23.6 %collective-permute-start.5 = (f32[2048,128]{1,0:T(8,128)S(1)}, f32[2048,128]{1,0:T(8,128)}, u32[]{:S(2)}, u32[]{:S(2)}) collective-permute-start(f32[2048,128]{1,0:T(8,128)S(1)} %dynamic-slice_add_fusion.4), channel_id=1, source_target_pairs={{0,1},{1,2},{2,3},{3,0},{4,5},{5,6},{6,7},{7,4},{8,9},{9,10},{10,1... | collective-permute-start | bytes 3145736 | tf_op jit(solution)/shard_map/ppermute | solution.py:31
  120.7 65.1 %copy-start.10 = (f32[128,512]{1,0:T(8,128)S(1)}, f32[128,512]{1,0:T(8,128)}, u32[]{:S(2)}) copy-start(f32[128,512]{1,0:T(8,128)} %param.10) | copy-start | bytes 786436
  120.7 141.3 %all-gather.2.cloned.1.call-start = ((), (), s32[]{:S(2)}) async-start(), calls=%async_computation.4 | async-start | bytes 2359296 | tf_op jit(solution)/shard_map/all_gather | solution.py:103
  122.5 12.2 %collective-permute-start = (f32[512,256]{1,0:T(8,128)S(1)}, f32[512,256]{1,0:T(8,128)S(1)}, u32[]{:S(2)}, u32[]{:S(2)}) collective-permute-start(f32[512,256]{1,0:T(8,128)S(1)} %constant_dynamic-slice_fusion.5), channel_id=1, source_target_pairs={{0,32},{32,0},{1,33},{33,1},{2,34},{34,2},{3,35},{35,3},{4,36},{36... | collective-permute-start | bytes 1572872 | tf_op jit(solution)/shard_map/ppermute | solution.py:45
  136.0 30.0 %collective-permute-start.1 = (f32[256,256]{1,0:T(8,128)S(1)}, f32[256,256]{1,0:T(8,128)S(1)}, u32[]{:S(2)}, u32[]{:S(2)}) collective-permute-start(f32[256,256]{1,0:T(8,128)S(1)} %constant_dynamic-slice_fusion.4), channel_id=1, source_target_pairs={{0,2},{1,3},{2,0},{3,1},{4,6},{5,7},{6,4},{7,5},{8,10},{9,11},{10,... | collective-permute-start | bytes 786440 | tf_op jit(solution)/shard_map/ppermute | solution.py:45
  163.3 5.4 %collective-permute-start.9 = (f32[128,256]{1,0:T(8,128)S(1)}, f32[128,256]{1,0:T(8,128)S(1)}, u32[]{:S(2)}, u32[]{:S(2)}) collective-permute-start(f32[128,256]{1,0:T(8,128)S(1)} %constant_dynamic-slice_fusion), channel_id=1, source_target_pairs={{0,32},{32,0},{1,33},{33,1},{2,34},{34,2},{3,35},{35,3},{4,36},{36... | collective-permute-start | bytes 393224 | tf_op jit(solution)/shard_map/ppermute | solution.py:45
  166.0 4.1 %collective-permute-start.2 = (f32[128,256]{1,0:T(8,128)S(1)}, f32[128,256]{1,0:T(8,128)S(1)}, u32[]{:S(2)}, u32[]{:S(2)}) collective-permute-start(f32[128,256]{1,0:T(8,128)S(1)} %constant_dynamic-slice_fusion.3), channel_id=1, source_target_pairs={{0,1},{1,0},{2,3},{3,2},{4,5},{5,4},{6,7},{7,6},{8,9},{9,8},{10,11... | collective-permute-start | bytes 393224 | tf_op jit(solution)/shard_map/ppermute | solution.py:45
  170.4 7.8 %collective-permute-start.10 = (f32[128,512]{1,0:T(8,128)S(1)}, f32[128,512]{1,0:T(8,128)S(1)}, u32[]{:S(2)}, u32[]{:S(2)}) collective-permute-start(f32[128,512]{1,0:T(8,128)S(1)} %fusion.7), channel_id=1, source_target_pairs={{0,64},{64,0},{128,192},{192,128},{1,65},{65,1},{129,193},{193,129... | collective-permute-start | bytes 786440 | tf_op jit(solution)/shard_map/ppermute | solution.py:91
  178.3 7.6 %collective-permute-start.11 = (f32[128,512]{1,0:T(8,128)S(1)}, f32[128,512]{1,0:T(8,128)S(1)}, u32[]{:S(2)}, u32[]{:S(2)}) collective-permute-start(f32[128,512]{1,0:T(8,128)S(1)} %add.259), channel_id=1, source_target_pairs={{0,128},{64,192},{128,0},{192,64},{1,129},{65,193},{129,1},{193,65... | collective-permute-start | bytes 786440 | tf_op jit(solution)/shard_map/ppermute | solution.py:92
  186.7 2.9 %collective-permute-start.12 = (bf16[128,128]{1,0:T(8,128)(2,1)S(1)}, bf16[128,128]{1,0:T(8,128)(2,1)S(1)}, u32[]{:S(2)}, u32[]{:S(2)}) collective-permute-start(bf16[128,128]{1,0:T(8,128)(2,1)S(1)} %get-tuple-element.28), channel_id=1, source_target_pairs={{0,1},{1,0},{2,3},{3,2},{4,5},{5,4},{6,7},{7,6},{8,9},{9,8},{10,11... | collective-permute-start | bytes 98312 | tf_op jit(solution)/shard_map/ppermute | solution.py:56
  189.6 4.7 %collective-permute-start.13 = (bf16[256,128]{1,0:T(8,128)(2,1)S(1)}, bf16[256,128]{1,0:T(8,128)(2,1)S(1)}, u32[]{:S(2)}, u32[]{:S(2)}) collective-permute-start(bf16[256,128]{1,0:T(8,128)(2,1)S(1)} %maximum_select_fusion.5), channel_id=1, source_target_pairs={{0,2},{1,3},{2,0},{3,1},{4,6},{5,7},{6,4},{7,5},{8,10},{9,11},{10,... | collective-permute-start | bytes 196616 | tf_op jit(solution)/shard_map/ppermute | solution.py:56
  194.3 21.8 %collective-permute-start.14 = (bf16[512,128]{1,0:T(8,128)(2,1)S(1)}, bf16[512,128]{1,0:T(8,128)(2,1)S(1)}, u32[]{:S(2)}, u32[]{:S(2)}) collective-permute-start(bf16[512,128]{1,0:T(8,128)(2,1)S(1)} %maximum_select_fusion.4), channel_id=1, source_target_pairs={{0,32},{32,0},{1,33},{33,1},{2,34},{34,2},{3,35},{35,3},{4,36},{36... | collective-permute-start | bytes 393224 | tf_op jit(solution)/shard_map/ppermute | solution.py:56
  214.9 5.5 %collective-permute-start.15 = (bf16[1024,128]{1,0:T(8,128)(2,1)S(1)}, bf16[1024,128]{1,0:T(8,128)(2,1)S(1)}, u32[]{:S(2)}, u32[]{:S(2)}) collective-permute-start(bf16[1024,128]{1,0:T(8,128)(2,1)S(1)} %all_gather.7), channel_id=1, source_target_pairs={{0,1},{1,0},{2,3},{3,2},{4,5},{5,4},{6,7},{7,6},{8,9},{9,8},{10,11... | collective-permute-start | bytes 786440 | tf_op jit(solution)/shard_map/ppermute | solution.py:56
  220.6 11.3 %collective-permute-start.16 = (bf16[2048,128]{1,0:T(8,128)(2,1)S(1)}, bf16[2048,128]{1,0:T(8,128)(2,1)S(1)}, u32[]{:S(2)}, u32[]{:S(2)}) collective-permute-start(bf16[2048,128]{1,0:T(8,128)(2,1)S(1)} %maximum_select_fusion.2), channel_id=1, source_target_pairs={{0,2},{1,3},{2,0},{3,1},{4,6},{5,7},{6,4},{7,5},{8,10},{9,11},{10,... | collective-permute-start | bytes 1572872 | tf_op jit(solution)/shard_map/ppermute | solution.py:56
  232.2 15.3 %collective-permute-start.17 = (bf16[4096,128]{1,0:T(8,128)(2,1)S(1)}, bf16[4096,128]{1,0:T(8,128)(2,1)S(1)}, u32[]{:S(2)}, u32[]{:S(2)}) collective-permute-start(bf16[4096,128]{1,0:T(8,128)(2,1)S(1)} %maximum_select_fusion.1), channel_id=1, source_target_pairs={{0,32},{32,0},{1,33},{33,1},{2,34},{34,2},{3,35},{35,3},{4,36},{36... | collective-permute-start | bytes 3145736 | tf_op jit(solution)/shard_map/ppermute | solution.py:56
  248.0 23.2 %collective-permute-start.19 = (bf16[8192,128]{1,0:T(8,128)(2,1)S(1)}, bf16[8192,128]{1,0:T(8,128)(2,1)}, u32[]{:S(2)}, u32[]{:S(2)}) collective-permute-start(bf16[8192,128]{1,0:T(8,128)(2,1)S(1)} %maximum_select_fusion), channel_id=1, source_target_pairs={{0,64},{64,0},{128,192},{192,128},{1,65},{65,1},{129,193},{193,129... | collective-permute-start | bytes 6291464 | tf_op jit(solution)/shard_map/ppermute | solution.py:109
  262.0 11.8 %collective-permute-start.18 = (bf16[8192,128]{1,0:T(8,128)(2,1)}, bf16[8192,128]{1,0:T(8,128)(2,1)}, u32[]{:S(2)}, u32[]{:S(2)}) collective-permute-start(bf16[8192,128]{1,0:T(8,128)(2,1)} %all-gather.2.cloned.1.call-done), channel_id=1, source_target_pairs={{0,64},{64,0},{128,192},{192,128},{1,65},{65,1},{129,193},{193,129... | collective-permute-start | bytes 6291464 | tf_op jit(solution)/shard_map/ppermute | solution.py:108
  (10 other events, 273.2 us)
Sparse Core Ops, SparseCore 0:
  22.7 98.6 reduce-scatter.2
  124.0 38.3 reduce-scatter.4
  217.0 42.8 all-gather.1

commit v6 on v4

--- a/solution.py
+++ b/solution.py
@@ -79,17 +79,25 @@
     grad_z = halving_scatter(grad_z, "y")
     grad_y = lax.psum_scatter(grad_y, "z", scatter_dimension=0, tiled=True)
     grad_y = halving_scatter(grad_y, "xh")
-    grad = jnp.concatenate([grad_z, grad_y], axis=1)
-    grad = grad * scale
-    drift = island_drift[0]
-    first = beta_one * moment1[0] + (1.0 - beta_one) * grad
-    second = beta_two * moment2[0] + (1.0 - beta_two) * grad * grad
-    step = first / (jnp.sqrt(second) + epsilon) + decay_rate * (global_params - drift)
-    pseudo = drift + inner_rate * step
+    drift_all = island_drift[0]
     pair_core = [(i, i ^ 1) for i in range(island_count)]
     pair_chip = [(i, i ^ 2) for i in range(island_count)]
-    summed = pseudo + lax.ppermute(pseudo, "island", pair_core)
-    summed = summed + lax.ppermute(summed, "island", pair_chip)
+    firsts, seconds, sums = [], [], []
+    for g, cs in ((grad_z, slice(0, cols)), (grad_y, slice(cols, None))):
+        g = g * scale
+        drift = drift_all[:, cs]
+        first = beta_one * moment1[0][:, cs] + (1.0 - beta_one) * g
+        second = beta_two * moment2[0][:, cs] + (1.0 - beta_two) * g * g
+        step = first / (jnp.sqrt(second) + epsilon) + decay_rate * (global_params[:, cs] - drift)
+        pseudo = drift + inner_rate * step
+        summed = pseudo + lax.ppermute(pseudo, "island", pair_core)
+        summed = summed + lax.ppermute(summed, "island", pair_chip)
+        firsts.append(first)
+        seconds.append(second)
+        sums.append(summed)
+    first = jnp.concatenate(firsts, axis=1)
+    second = jnp.concatenate(seconds, axis=1)
+    summed = jnp.concatenate(sums, axis=1)
     mean = summed / island_count
     new_momentum = nesterov * momentum + mean
     new_global = global_params - outer_rate * (mean + nesterov * new_momentum)

time: 282 us -> 282 us (level)
  waiting for transfers between devices: 175 us -> 178 us
    reduce_scatter x1, waiting for transfers between devices: 0.96 us -> 5.43 us  [per_device(): grad_z = lax.psum_scatter(part_z, 'z', scatter_dimension=0, tiled=True)]
    ppermute x6, waiting for transfers between devices: 61.8 us -> 57.9 us  [ring_scatter(): acc = lax.ppermute(acc, axis, perm) + pick(me - sign * (2 + s) + 2 * n)]
    ppermute x1 -> x2, waiting for transfers between devices: 6.77 us -> 5.91 us  [per_device(): summed = summed + lax.ppermute(summed, 'island', pair_chip)]
    ppermute x1 -> x2, starting transfers between devices: 6.25 us -> 6.55 us  [per_device(): summed = pseudo + lax.ppermute(pseudo, 'island', pair_core)]
  transfers between devices with their start and end apart: 19 -> 21, of which waited for: 16 -> 18; matrix products, arithmetic and copies ran while one was open for 10% -> 10% of each run, Pallas kernels for 0% -> 0%
where the time goes in v6:
time: 282 us
  waiting for transfers between devices  178 us (63%)
  starting transfers between devices  34.4 us (12%)
  local copies, waits for them, and re-layouts  24.6 us (9%)
  other arithmetic  16.6 us (6%)
  matrix products  14 us (5%)
  between operations  14 us (5%)
    ppermute x6, waiting for transfers between devices, ring_scatter(): acc = lax.ppermute(acc, axis, perm) + pick(me - sign * (2 + s) + 2 * n)  57.9 us
    all_gather x1, waiting for transfers between devices, per_device(): own_full = lax.all_gather(own_full, 'z', axis=0, tiled=True)  55.7 us
    reduce_scatter x1, waiting for transfers between devices, per_device(): grad_y = lax.psum_scatter(grad_y, 'z', scatter_dimension=0, tiled=True)  21.9 us
    ppermute x4, waiting for transfers between devices, halving_scatter(): recv = lax.ppermute(send, axis, [(i, i ^ bit) for i in range(n)])  14 us
    unnamed x24, local copies, waits for them, and re-layouts  11.2 us
    ppermute x4, starting transfers between devices, halving_scatter(): recv = lax.ppermute(send, axis, [(i, i ^ bit) for i in range(n)])  10 us
    add x6, other arithmetic, ring_scatter(): acc = lax.ppermute(acc, axis, perm) + pick(me - sign * (2 + s) + 2 * n)  9.94 us
    ppermute x3, waiting for transfers between devices, doubling_gather(): recv = lax.ppermute(x, axis, [(i, i ^ bit) for i in range(n)])  9.92 us
  transfers between devices with their start and end apart: 21, of which 18 were waited for; matrix products, arithmetic and copies ran while one was open for 10% of the time, Pallas kernels for 0%

profile of v6, /device:TPU:1, one launch (start us, length us, event | category | flops | bytes accessed | tf_op | source)
XLA Modules:
  0.0 281.6 jit_solution(5232345041653849499)
XLA Ops:
  7.2 6.4 %copy.19 = bf16[256,8192]{0,1:T(8,128)(2,1)} copy(bf16[256,8192]{1,0:T(8,128)(2,1)} %param.7) | data formatting | bytes 8388608 | tf_op args[0]
  13.6 2.5 copy.20
  18.1 4.5 %fusion.8 = f32[8192,256]{1,0:T(8,128)} fusion(bf16[256,8192]{0,1:T(8,128)(2,1)S(1)} %bitcast.24, bf16[256,512]{1,0:T(8,128)(2,1)S(1)} %copy-done.6), kind=kOutput, calls=%fused_computation.39 | convolution fusion | flops 1073741824 | bytes 12713984 | tf_op jit(solution)/shard_map/dot_general | solution.py:74
  22.7 4.7 %copy.21 = bf16[256,4,8,2,128]{0,4,3,2,1:T(8,128)(2,1)} copy(bf16[256,4,8,2,128]{0,4,1,2,3:T(8,128)(2,1)} %bitcast.28) | data formatting | bytes 8388608 | tf_op jit(solution)/shard_map/transpose | solution.py:71
  27.4 3.4 %fusion.6 = f32[8192,256]{1,0:T(8,128)S(1)} fusion(bf16[256,8192]{0,1:T(8,128)(2,1)} %bitcast.29, bf16[256,512]{1,0:T(8,128)(2,1)S(1)} %copy-done.6), kind=kOutput, calls=%fused_computation.35 | convolution fusion | flops 1073741824 | bytes 12713984 | tf_op jit(solution)/shard_map/dot_general | solution.py:75
  30.8 2.5 fusion.14
  40.4 19.6 %collective-permute-done.5 = f32[2048,128]{1,0:T(8,128)S(1)} collective-permute-done((f32[2048,128]{1,0:T(8,128)S(1)}, f32[2048,128]{1,0:T(8,128)S(1)}, u32[]{:S(2)}, u32[]{:S(2)}) %collective-permute-start.5) | collective-permute-done | bytes 1048608 | tf_op jit(solution)/shard_map/ppermute | solution.py:31
  63.0 2.6 dynamic-slice_add_fusion.2
  67.2 18.0 %collective-permute-done.6 = f32[2048,128]{1,0:T(8,128)S(1)} collective-permute-done((f32[2048,128]{1,0:T(8,128)S(1)}, f32[2048,128]{1,0:T(8,128)S(1)}, u32[]{:S(2)}, u32[]{:S(2)}) %collective-permute-start.6) | collective-permute-done | bytes 1048608 | tf_op jit(solution)/shard_map/ppermute | solution.py:31
  92.3 17.0 %collective-permute-done.7 = f32[2048,128]{1,0:T(8,128)S(1)} collective-permute-done((f32[2048,128]{1,0:T(8,128)S(1)}, f32[2048,128]{1,0:T(8,128)S(1)}, u32[]{:S(2)}, u32[]{:S(2)}) %collective-permute-start.7) | collective-permute-done | bytes 1048608 | tf_op jit(solution)/shard_map/ppermute | solution.py:31
  116.0 5.4 %reduce-scatter.3.cloned.1.call-done = f32[1024,256]{1,0:T(8,128)} async-done(((f32[8192,256]{1,0:T(8,128)}), f32[1024,256]{1,0:T(8,128)}) %reduce-scatter.3.cloned.1.call-update) | async-done | bytes 1048592 | tf_op jit(solution)/shard_map/reduce_scatter | solution.py:76
  122.5 2.8 collective-permute-start
  125.3 11.5 %collective-permute-done = f32[512,256]{1,0:T(8,128)S(1)} collective-permute-done((f32[512,256]{1,0:T(8,128)S(1)}, f32[512,256]{1,0:T(8,128)S(1)}, u32[]{:S(2)}, u32[]{:S(2)}) %collective-permute-start) | collective-permute-done | bytes 524320 | tf_op jit(solution)/shard_map/ppermute | solution.py:45
  138.0 2.8 collective-permute-start.1
  140.8 21.9 %reduce-scatter.5.cloned.1.call-done = f32[256,256]{1,0:T(8,128)} async-done(((f32[2048,256]{1,0:T(8,128)}), f32[256,256]{1,0:T(8,128)}) %reduce-scatter.5.cloned.1.call-update) | async-done | bytes 262160 | tf_op jit(solution)/shard_map/reduce_scatter | solution.py:80
  163.7 2.8 %collective-permute-start.11 = (f32[128,256]{1,0:T(8,128)S(1)}, f32[128,256]{1,0:T(8,128)S(1)}, u32[]{:S(2)}, u32[]{:S(2)}) collective-permute-start(f32[128,256]{1,0:T(8,128)S(1)} %constant_dynamic-slice_fusion), channel_id=1, source_target_pairs={{0,32},{32,0},{1,33},{33,1},{2,34},{34,2},{3,35},{35,3},{4,36},{36... | collective-permute-start | bytes 393224 | tf_op jit(solution)/shard_map/ppermute | solution.py:45
  171.8 6.5 %collective-permute-start.3 = (f32[128,256]{1,0:T(8,128)S(1)}, f32[128,256]{1,0:T(8,128)S(1)}, u32[]{:S(2)}, u32[]{:S(2)}) collective-permute-start(f32[128,256]{1,0:T(8,128)S(1)} %get-tuple-element.22), channel_id=1, source_target_pairs={{0,64},{64,0},{128,192},{192,128},{1,65},{65,1},{129,193},{193,129... | collective-permute-start | bytes 393224 | tf_op jit(solution)/shard_map/ppermute | solution.py:93
  180.9 3.1 %collective-permute-done.4 = f32[128,256]{1,0:T(8,128)S(1)} collective-permute-done((f32[128,256]{1,0:T(8,128)S(1)}, f32[128,256]{1,0:T(8,128)S(1)}, u32[]{:S(2)}, u32[]{:S(2)}) %collective-permute-start.4) | collective-permute-done | bytes 131104 | tf_op jit(solution)/shard_map/ppermute | solution.py:94
  184.1 2.8 collective-permute-done.13
  190.9 3.1 %collective-permute-start.15 = (bf16[256,256]{1,0:T(8,128)(2,1)S(1)}, bf16[256,256]{1,0:T(8,128)(2,1)S(1)}, u32[]{:S(2)}, u32[]{:S(2)}) collective-permute-start(bf16[256,256]{1,0:T(8,128)(2,1)S(1)} %maximum_select_fusion.2), channel_id=1, source_target_pairs={{0,2},{1,3},{2,0},{3,1},{4,6},{5,7},{6,4},{7,5},{8,10},{9,11},{10,... | collective-permute-start | bytes 393224 | tf_op jit(solution)/shard_map/ppermute | solution.py:56
  197.5 5.8 %collective-permute-done.16 = bf16[512,256]{1,0:T(8,128)(2,1)S(1)} collective-permute-done((bf16[512,256]{1,0:T(8,128)(2,1)S(1)}, bf16[512,256]{1,0:T(8,128)(2,1)S(1)}, u32[]{:S(2)}, u32[]{:S(2)}) %collective-permute-start.16) | collective-permute-done | bytes 262176 | tf_op jit(solution)/shard_map/ppermute | solution.py:56
  204.4 55.7 %all-gather.2.cloned.1.call-done = bf16[8192,256]{1,0:T(8,128)(2,1)} async-done(((bf16[1024,256]{1,0:T(8,128)(2,1)}), bf16[8192,256]{1,0:T(8,128)(2,1)}) %all-gather.2.cloned.1.call-update) | async-done | bytes 4194320 | tf_op jit(solution)/shard_map/all_gather | solution.py:110
  261.8 6.3 %collective-permute-done.17 = bf16[8192,256]{1,0:T(8,128)(2,1)} collective-permute-done((bf16[8192,256]{1,0:T(8,128)(2,1)}, bf16[8192,256]{1,0:T(8,128)(2,1)}, u32[]{:S(2)}, u32[]{:S(2)}) %collective-permute-start.17) | collective-permute-done | bytes 4194336 | tf_op jit(solution)/shard_map/ppermute | solution.py:111
  268.1 4.8 %fusion.1 = bf16[256,256]{1,0:T(8,128)(2,1)S(1)} fusion(bf16[8192,256]{1,0:T(8,128)(2,1)} %collective-permute-done.17, bf16[256,8192]{0,1:T(8,128)(2,1)} %bitcast.25), kind=kOutput, calls=%fused_computation.4 | convolution fusion | flops 1073872896 | bytes 8519680 | tf_op jit(solution)/shard_map/dot_general | solution.py:113
  (79 shorter events, 51.1 us)
Async XLA Ops:
  7.2 114.3 %reduce-scatter.3.cloned.1.call-start = ((), (), s32[]{:S(2)}) async-start(), calls=%async_computation.2 | async-start | bytes 9437184 | tf_op jit(solution)/shard_map/reduce_scatter | solution.py:76
  22.7 140.1 %reduce-scatter.5.cloned.1.call-start = ((), (), s32[]{:S(2)}) async-start(), calls=%async_computation.3 | async-start | bytes 2359296 | tf_op jit(solution)/shard_map/reduce_scatter | solution.py:80
  35.3 24.7 %collective-permute-start.5 = (f32[2048,128]{1,0:T(8,128)S(1)}, f32[2048,128]{1,0:T(8,128)S(1)}, u32[]{:S(2)}, u32[]{:S(2)}) collective-permute-start(f32[2048,128]{1,0:T(8,128)S(1)} %constant_dynamic-slice_fusion.2), channel_id=1, source_target_pairs={{0,1},{1,2},{2,3},{3,0},{4,5},{5,6},{6,7},{7,4},{8,9},{9,10},{10,1... | collective-permute-start | bytes 3145736 | tf_op jit(solution)/shard_map/ppermute | solution.py:31
  39.1 23.8 %collective-permute-start.8 = (f32[2048,128]{1,0:T(8,128)S(1)}, f32[2048,128]{1,0:T(8,128)}, u32[]{:S(2)}, u32[]{:S(2)}) collective-permute-start(f32[2048,128]{1,0:T(8,128)S(1)} %constant_dynamic-slice_fusion.1), channel_id=1, source_target_pairs={{0,3},{1,0},{2,1},{3,2},{4,7},{5,4},{6,5},{7,6},{8,11},{9,8},{10,9... | collective-permute-start | bytes 3145736 | tf_op jit(solution)/shard_map/ppermute | solution.py:31
  61.3 23.9 %collective-permute-start.6 = (f32[2048,128]{1,0:T(8,128)S(1)}, f32[2048,128]{1,0:T(8,128)S(1)}, u32[]{:S(2)}, u32[]{:S(2)}) collective-permute-start(f32[2048,128]{1,0:T(8,128)S(1)} %dynamic-slice_add_fusion.5), channel_id=1, source_target_pairs={{0,1},{1,2},{2,3},{3,0},{4,5},{5,6},{6,7},{7,4},{8,9},{9,10},{10,1... | collective-permute-start | bytes 3145736 | tf_op jit(solution)/shard_map/ppermute | solution.py:31
  65.6 23.1 %collective-permute-start.9 = (f32[2048,128]{1,0:T(8,128)}, f32[2048,128]{1,0:T(8,128)}, u32[]{:S(2)}, u32[]{:S(2)}) collective-permute-start(f32[2048,128]{1,0:T(8,128)} %dynamic-slice_add_fusion.2), channel_id=1, source_target_pairs={{0,3},{1,0},{2,1},{3,2},{4,7},{5,4},{6,5},{7,6},{8,11},{9,8},{10,9... | collective-permute-start | bytes 3145736 | tf_op jit(solution)/shard_map/ppermute | solution.py:31
  86.6 22.7 %collective-permute-start.7 = (f32[2048,128]{1,0:T(8,128)S(1)}, f32[2048,128]{1,0:T(8,128)S(1)}, u32[]{:S(2)}, u32[]{:S(2)}) collective-permute-start(f32[2048,128]{1,0:T(8,128)S(1)} %dynamic-slice_add_fusion.4), channel_id=1, source_target_pairs={{0,1},{1,2},{2,3},{3,0},{4,5},{5,6},{6,7},{7,4},{8,9},{9,10},{10,1... | collective-permute-start | bytes 3145736 | tf_op jit(solution)/shard_map/ppermute | solution.py:31
  90.4 22.4 %collective-permute-start.10 = (f32[2048,128]{1,0:T(8,128)S(1)}, f32[2048,128]{1,0:T(8,128)}, u32[]{:S(2)}, u32[]{:S(2)}) collective-permute-start(f32[2048,128]{1,0:T(8,128)S(1)} %dynamic-slice_add_fusion.1), channel_id=1, source_target_pairs={{0,3},{1,0},{2,1},{3,2},{4,7},{5,4},{6,5},{7,6},{8,11},{9,8},{10,9... | collective-permute-start | bytes 3145736 | tf_op jit(solution)/shard_map/ppermute | solution.py:31
  115.9 54.7 %copy-start.9 = (f32[1,128,512]{2,1,0:T(8,128)S(1)}, f32[1,128,512]{2,1,0:T(8,128)}, u32[]{:S(2)}) copy-start(f32[1,128,512]{2,1,0:T(8,128)} %param.12) | copy-start | bytes 786436
  116.0 144.1 %all-gather.2.cloned.1.call-start = ((), (), s32[]{:S(2)}) async-start(), calls=%async_computation.4 | async-start | bytes 4718592 | tf_op jit(solution)/shard_map/all_gather | solution.py:110
  116.0 70.9 %copy-start.10 = (f32[128,512]{1,0:T(8,128)S(1)}, f32[128,512]{1,0:T(8,128)}, u32[]{:S(2)}) copy-start(f32[128,512]{1,0:T(8,128)} %param.10) | copy-start | bytes 786436
  122.5 14.3 %collective-permute-start = (f32[512,256]{1,0:T(8,128)S(1)}, f32[512,256]{1,0:T(8,128)S(1)}, u32[]{:S(2)}, u32[]{:S(2)}) collective-permute-start(f32[512,256]{1,0:T(8,128)S(1)} %constant_dynamic-slice_fusion.5), channel_id=1, source_target_pairs={{0,32},{32,0},{1,33},{33,1},{2,34},{34,2},{3,35},{35,3},{4,36},{36... | collective-permute-start | bytes 1572872 | tf_op jit(solution)/shard_map/ppermute | solution.py:45
  138.0 28.5 %collective-permute-start.1 = (f32[256,256]{1,0:T(8,128)S(1)}, f32[256,256]{1,0:T(8,128)S(1)}, u32[]{:S(2)}, u32[]{:S(2)}) collective-permute-start(f32[256,256]{1,0:T(8,128)S(1)} %constant_dynamic-slice_fusion.4), channel_id=1, source_target_pairs={{0,2},{1,3},{2,0},{3,1},{4,6},{5,7},{6,4},{7,5},{8,10},{9,11},{10,... | collective-permute-start | bytes 786440 | tf_op jit(solution)/shard_map/ppermute | solution.py:45
  163.7 5.4 %collective-permute-start.11 = (f32[128,256]{1,0:T(8,128)S(1)}, f32[128,256]{1,0:T(8,128)S(1)}, u32[]{:S(2)}, u32[]{:S(2)}) collective-permute-start(f32[128,256]{1,0:T(8,128)S(1)} %constant_dynamic-slice_fusion), channel_id=1, source_target_pairs={{0,32},{32,0},{1,33},{33,1},{2,34},{34,2},{3,35},{35,3},{4,36},{36... | collective-permute-start | bytes 393224 | tf_op jit(solution)/shard_map/ppermute | solution.py:45
  166.6 4.1 %collective-permute-start.2 = (f32[128,256]{1,0:T(8,128)S(1)}, f32[128,256]{1,0:T(8,128)S(1)}, u32[]{:S(2)}, u32[]{:S(2)}) collective-permute-start(f32[128,256]{1,0:T(8,128)S(1)} %constant_dynamic-slice_fusion.3), channel_id=1, source_target_pairs={{0,1},{1,0},{2,3},{3,2},{4,5},{5,4},{6,7},{7,6},{8,9},{9,8},{10,11... | collective-permute-start | bytes 393224 | tf_op jit(solution)/shard_map/ppermute | solution.py:45
  171.8 7.4 %collective-permute-start.3 = (f32[128,256]{1,0:T(8,128)S(1)}, f32[128,256]{1,0:T(8,128)S(1)}, u32[]{:S(2)}, u32[]{:S(2)}) collective-permute-start(f32[128,256]{1,0:T(8,128)S(1)} %get-tuple-element.22), channel_id=1, source_target_pairs={{0,64},{64,0},{128,192},{192,128},{1,65},{65,1},{129,193},{193,129... | collective-permute-start | bytes 393224 | tf_op jit(solution)/shard_map/ppermute | solution.py:93
  178.3 1.6 collective-permute-start.12
  179.3 4.8 %collective-permute-start.4 = (f32[128,256]{1,0:T(8,128)S(1)}, f32[128,256]{1,0:T(8,128)S(1)}, u32[]{:S(2)}, u32[]{:S(2)}) collective-permute-start(f32[128,256]{1,0:T(8,128)S(1)} %add.237), channel_id=1, source_target_pairs={{0,128},{64,192},{128,0},{192,64},{1,129},{65,193},{129,1},{193,65... | collective-permute-start | bytes 393224 | tf_op jit(solution)/shard_map/ppermute | solution.py:94
  179.9 7.0 %collective-permute-start.13 = (f32[128,256]{1,0:T(8,128)S(1)}, f32[128,256]{1,0:T(8,128)S(1)}, u32[]{:S(2)}, u32[]{:S(2)}) collective-permute-start(f32[128,256]{1,0:T(8,128)S(1)} %add.274), channel_id=1, source_target_pairs={{0,128},{64,192},{128,0},{192,64},{1,129},{65,193},{129,1},{193,65... | collective-permute-start | bytes 393224 | tf_op jit(solution)/shard_map/ppermute | solution.py:94
  187.7 85.2 %copy-start.5 = (f32[128,512]{1,0:T(8,128)}, f32[128,512]{1,0:T(8,128)S(1)}, u32[]{:S(2)}) copy-start(f32[128,512]{1,0:T(8,128)S(1)} %get-tuple-element.20) | copy-start | bytes 786436
  187.7 3.2 %collective-permute-start.14 = (bf16[128,256]{1,0:T(8,128)(2,1)S(1)}, bf16[128,256]{1,0:T(8,128)(2,1)S(1)}, u32[]{:S(2)}, u32[]{:S(2)}) collective-permute-start(bf16[128,256]{1,0:T(8,128)(2,1)S(1)} %dynamic-slice_convert_fusion), channel_id=1, source_target_pairs={{0,1},{1,0},{2,3},{3,2},{4,5},{5,4},{6,7},{7,6},{8,9},{9,8},{10,11... | collective-permute-start | bytes 196616 | tf_op jit(solution)/shard_map/ppermute | solution.py:56
  190.9 5.5 %collective-permute-start.15 = (bf16[256,256]{1,0:T(8,128)(2,1)S(1)}, bf16[256,256]{1,0:T(8,128)(2,1)S(1)}, u32[]{:S(2)}, u32[]{:S(2)}) collective-permute-start(bf16[256,256]{1,0:T(8,128)(2,1)S(1)} %maximum_select_fusion.2), channel_id=1, source_target_pairs={{0,2},{1,3},{2,0},{3,1},{4,6},{5,7},{6,4},{7,5},{8,10},{9,11},{10,... | collective-permute-start | bytes 393224 | tf_op jit(solution)/shard_map/ppermute | solution.py:56
  196.5 6.8 %collective-permute-start.16 = (bf16[512,256]{1,0:T(8,128)(2,1)S(1)}, bf16[512,256]{1,0:T(8,128)(2,1)S(1)}, u32[]{:S(2)}, u32[]{:S(2)}) collective-permute-start(bf16[512,256]{1,0:T(8,128)(2,1)S(1)} %maximum_select_fusion.1), channel_id=1, source_target_pairs={{0,32},{32,0},{1,33},{33,1},{2,34},{34,2},{3,35},{35,3},{4,36},{36... | collective-permute-start | bytes 786440 | tf_op jit(solution)/shard_map/ppermute | solution.py:56
  260.1 8.0 %collective-permute-start.17 = (bf16[8192,256]{1,0:T(8,128)(2,1)}, bf16[8192,256]{1,0:T(8,128)(2,1)}, u32[]{:S(2)}, u32[]{:S(2)}) collective-permute-start(bf16[8192,256]{1,0:T(8,128)(2,1)} %all-gather.2.cloned.1.call-done), channel_id=1, source_target_pairs={{0,64},{64,0},{128,192},{192,128},{1,65},{65,1},{129,193},{193,129... | collective-permute-start | bytes 12582920 | tf_op jit(solution)/shard_map/ppermute | solution.py:111
  (8 other events, 194.8 us)
Sparse Core Ops, SparseCore 0:
  22.8 98.6 reduce-scatter.2
  124.0 38.6 reduce-scatter.4
  204.5 55.5 all-gather.1
